TPU v7x, 512 devices: a whole 4x4x16 slice. The times are simulated.
512 devices in a mesh: strip: 512 (over z, y, x, core).
Axes of the slice: x: 4, y: 4, z: 16, core: 2. Of those that a mesh axis runs over, the one named last changes fastest.
Arguments:
- velocity: float32 [2, 128, 2048, 768], P(None, None, 'strip'), may hold values from -100 to 100
Outputs:
- spatial_modes: float32 [128, 2048, 768], P(None, 'strip')
- triangle: float32 [128, 128], replicated
All inputs are finite; a program needn't handle non-finite values.
Results may differ from a plain program's by a relative error of at most 0.000094.
Values sent between devices are 32-bit elements; how exact they have to be, the bound alone decides.
No kernel may reach another device: no remote copies, remote signals or barrier semaphores. Data moves between devices by JAX's collectives and lax.ppermute only.
A program may use at most 128 MiB of HBM per device.

v0:
```python
import jax
import jax.numpy as jnp
from jax import lax
from jax.sharding import PartitionSpec as P


def extended(array, sides, width):
    for axis, dim in sides:
        size, length = (lax.axis_size(axis), array.shape[dim])
        up = [(i, (i + 1) % size) for i in range(size)]
        down = [(j, i) for i, j in up]
        last = lax.slice_in_dim(array, length - width, length, axis=dim)
        initial = lax.slice_in_dim(array, 0, width, axis=dim)
        before = lax.ppermute(last, axis, up)
        after = lax.ppermute(initial, axis, down)
        array = jnp.concatenate([before, array, after], axis=dim)
    return array


def along_second(field):
    return (
        8.0 * (jnp.roll(field, -1, 2) - jnp.roll(field, 1, 2))
        - (jnp.roll(field, -2, 2) - jnp.roll(field, 2, 2))
    ) / 12.0


def stencil_rows(padded, row_count):
    return 8.0 * (padded[:, 3 : row_count + 3] - padded[:, 1 : row_count + 1]) - (
        padded[:, 4 : row_count + 4] - padded[:, 0:row_count]
    )


def local(velocity):
    snap_count = velocity.shape[1]
    row_count = velocity.shape[2]
    col_count = velocity.shape[3]
    total_cells = row_count * lax.axis_size("strip") * col_count
    comp_u = velocity[0]
    comp_v = velocity[1]
    padded = extended(comp_v, (("strip", 1),), 2)
    v_first = stencil_rows(padded, row_count) / 12.0
    vorticity = v_first - along_second(comp_u)
    flattened = vorticity.reshape(snap_count, row_count * col_count)
    local_gram = (
        jnp.dot(
            flattened,
            flattened.T,
            precision=lax.Precision.HIGHEST,
            preferred_element_type=jnp.float32,
        )
        / total_cells
    )
    gram = lax.psum(local_gram, "strip")
    lower = jnp.linalg.cholesky(gram)
    identity = jnp.eye(snap_count, dtype=jnp.float32)
    inverse_lower = lax.linalg.triangular_solve(lower, identity, left_side=True, lower=True)
    spatial_modes = jnp.dot(
        inverse_lower,
        flattened,
        precision=lax.Precision.HIGHEST,
        preferred_element_type=jnp.float32,
    )
    return (spatial_modes.reshape(snap_count, row_count, col_count), lower.T)


def solution(mesh):
    return jax.shard_map(
        local,
        mesh=mesh,
        in_specs=(P(None, None, "strip", None),),
        out_specs=(P(None, "strip", None), P()),
        check_vma=False,
    )
```

profile of v0, /device:TPU:1, one launch (start us, length us, event | category | flops | bytes accessed | tf_op | source)
XLA Modules:
  0.0 519.4 jit_solution(6703230414431210953)
XLA Ops:
  7.2 0.0 all-reduce.2.cloned.1.call-start
  7.2 2.4 slice_bitcast_fusion
  9.6 0.6 fusion.26
  10.2 8.8 %collective-permute-start = (f32[128,2,768]{2,1,0:T(2,128)S(1)}, f32[128,2,768]{2,1,0:T(2,128)S(1)}, u32[]{:S(2)}, u32[]{:S(2)}) collective-permute-start(f32[128,2,768]{2,1,0:T(2,128)S(1)} %get-tuple-element.14), channel_id=1, source_target_pairs={{1,0},{2,1},{3,2},{4,3},{5,4},{6,5},{7,6},{8,7},{9,8},{10,9},{11,1... | collective-permute-start | bytes 2359304 | tf_op jit(solution)/shard_map/ppermute | solution.py:15
  19.0 1.9 collective-permute-start.1
  21.0 0.2 fusion.24
  21.2 0.2 fusion.22
  21.4 0.9 fusion.25
  22.3 0.9 fusion.23
  23.2 1.2 collective-permute-done
  24.4 6.5 %collective-permute-done.1 = f32[128,2,768]{2,1,0:T(2,128)S(1)} collective-permute-done((f32[128,2,768]{2,1,0:T(2,128)S(1)}, f32[128,2,768]{2,1,0:T(2,128)S(1)}, u32[]{:S(2)}, u32[]{:S(2)}) %collective-permute-start.1) | collective-permute-done | bytes 786464 | tf_op jit(solution)/shard_map/ppermute | solution.py:14
  30.9 5.1 fusion.5
  36.0 2.3 fusion.16
  38.3 0.0 all-reduce.2.cloned.1.call-update
  38.3 0.3 copy.12
  38.6 0.5 copy.7
  39.1 444.1 %all-reduce.2.cloned.1.call-done = f32[128,128]{0,1:T(8,128)} async-done(((f32[128,128]{0,1:T(8,128)}), f32[128,128]{0,1:T(8,128)}) %all-reduce.2.cloned.1.call-update) | async-done | bytes 65552 | tf_op jit(solution)/shard_map/psum | solution.py:53
  483.2 0.9 copy.6
  484.1 0.9 fusion.20
  485.0 11.7 %cholesky.17 = f32[128,128]{1,0:T(8,128)S(1)} custom-call(f32[128,128]{1,0:T(8,128)S(1)} %fusion.20), custom_call_target="Cholesky" | custom-call | tf_op jit(solution)/shard_map/jit(cholesky)/cholesky | solution.py:54
  496.8 0.6 compare_reduce_fusion
  497.4 0.7 fusion.21
  498.1 9.8 %custom-call.6 = f32[1,128,128]{1,2,0:T(8,128)S(1)} custom-call(f32[1,128,128]{2,1,0:T(8,128)S(1)} %get-tuple-element.17), custom_call_target="InvertDiagBlocksLowerTriangular" | custom-call | tf_op jit(solution)/shard_map/triangular_solve | solution.py:56
  507.9 0.2 convolution_bitcast_fusion
  508.1 1.5 fusion.27
  509.6 2.2 copy.8
  511.8 0.7 copy.9
  (1 shorter events, 0.0 us)
Async XLA Ops:
  7.2 476.1 %all-reduce.2.cloned.1.call-start = ((), (), s32[]{:S(2)}) async-start(), calls=%async_computation | async-start | bytes 131072 | tf_op jit(solution)/shard_map/psum | solution.py:53
  10.2 14.2 %collective-permute-start = (f32[128,2,768]{2,1,0:T(2,128)S(1)}, f32[128,2,768]{2,1,0:T(2,128)S(1)}, u32[]{:S(2)}, u32[]{:S(2)}) collective-permute-start(f32[128,2,768]{2,1,0:T(2,128)S(1)} %get-tuple-element.14), channel_id=1, source_target_pairs={{1,0},{2,1},{3,2},{4,3},{5,4},{6,5},{7,6},{8,7},{9,8},{10,9},{11,1... | collective-permute-start | bytes 2359304 | tf_op jit(solution)/shard_map/ppermute | solution.py:15
  19.0 11.9 %collective-permute-start.1 = (f32[128,2,768]{2,1,0:T(2,128)S(1)}, f32[128,2,768]{2,1,0:T(2,128)S(1)}, u32[]{:S(2)}, u32[]{:S(2)}) collective-permute-start(f32[128,2,768]{2,1,0:T(2,128)S(1)} %get-tuple-element.15), channel_id=1, source_target_pairs={{0,1},{1,2},{2,3},{3,4},{4,5},{5,6},{6,7},{7,8},{8,9},{9,10},{10,1... | collective-permute-start | bytes 2359304 | tf_op jit(solution)/shard_map/ppermute | solution.py:14
Sparse Core Ops, SparseCore 0:
  38.5 444.7 all-reduce.1
where the time goes:
time: 520 us; the launch traced here: 519 us
  waiting for transfers between devices  452 us (87%)
  other arithmetic  28.8 us (6%)
  between operations  14.1 us (3%)
  starting transfers between devices  10.7 us (2%)
  local copies, waits for them, and re-layouts  9.79 us (2%)
    psum x1, waiting for transfers between devices, local(): gram = lax.psum(local_gram, 'strip')  444 us
    another operation x3, other arithmetic, local(): lower = jnp.linalg.cholesky(gram)  12.4 us
  transfers between devices with their start and end apart: 3, of which 3 were waited for; matrix products, arithmetic and copies ran while one was open for 1% of the time, Pallas kernels for 0%

commit v1 on v0

--- a/solution.py
+++ b/solution.py
@@ -15,6 +15,16 @@
         after = lax.ppermute(initial, axis, down)
         array = jnp.concatenate([before, array, after], axis=dim)
     return array
+
+
+def butterfly_sum(value, axis):
+    size = lax.axis_size(axis)
+    bit = 1
+    while bit < size:
+        pairs = [(i, i ^ bit) for i in range(size)]
+        value = value + lax.ppermute(value, axis, pairs)
+        bit *= 2
+    return value
 
 
 def along_second(field):
@@ -50,7 +60,7 @@
         )
         / total_cells
     )
-    gram = lax.psum(local_gram, "strip")
+    gram = butterfly_sum(local_gram, "strip")
     lower = jnp.linalg.cholesky(gram)
     identity = jnp.eye(snap_count, dtype=jnp.float32)
     inverse_lower = lax.linalg.triangular_solve(lower, identity, left_side=True, lower=True)

time: 520 us -> 143 us (0.28)
  the two profiles are of different devices: /device:TPU:1 before, /device:TPU:8 now
where the time goes in v1:
time: 143 us; the launch traced here: 142 us
  waiting for transfers between devices  56 us (39%)
  starting transfers between devices  45.2 us (32%)
  other arithmetic  27.8 us (19%)
  local copies, waits for them, and re-layouts  8.95 us (6%)
  matrix products  3.43 us (2%)
    ppermute x9, waiting for transfers between devices, butterfly_sum(): value = value + lax.ppermute(value, axis, pairs)  44.7 us
    ppermute x9, starting transfers between devices, butterfly_sum(): value = value + lax.ppermute(value, axis, pairs)  39.3 us
    another operation x3, other arithmetic, local(): lower = jnp.linalg.cholesky(gram)  12.4 us
    another operation x1, other arithmetic, local(): lax.linalg.triangular_solve(lower, identity, left_side=True, lower=True)  9.81 us
    ppermute x1, waiting for transfers between devices, extended(): before = lax.ppermute(last, axis, up)  5.93 us
    ppermute x1, waiting for transfers between devices, extended(): after = lax.ppermute(initial, axis, down)  5.33 us
    sub x1, other arithmetic, local(): vorticity = v_first - along_second(comp_u)  4.88 us
    ppermute x1, starting transfers between devices, extended(): after = lax.ppermute(initial, axis, down)  3.99 us
  transfers between devices with their start and end apart: 11, of which 11 were waited for; matrix products, arithmetic and copies ran while one was open for 2% of the time, Pallas kernels for 0%

profile of v1, /device:TPU:8, one launch (start us, length us, event | category | flops | bytes accessed | tf_op | source)
XLA Modules:
  0.0 142.3 jit_solution(9141839016156101312)
XLA Ops:
  0.6 2.4 %slice_bitcast_fusion = (f32[128,4,768]{2,1,0:T(4,128)S(1)}, f32[128,4,768]{2,1,0:T(4,128)S(1)}) fusion(f32[2,128,4,768]{3,2,1,0:T(4,128)} %param.1), kind=kLoop, calls=%fused_computation.21 | loop fusion | bytes 6291456 | tf_op jit(solution)/shard_map/squeeze | solution.py:48
  3.1 0.6 fusion.26
  3.7 4.0 %collective-permute-start = (f32[128,2,768]{2,1,0:T(2,128)S(1)}, f32[128,2,768]{2,1,0:T(2,128)S(1)}, u32[]{:S(2)}, u32[]{:S(2)}) collective-permute-start(f32[128,2,768]{2,1,0:T(2,128)S(1)} %get-tuple-element.14), channel_id=1, source_target_pairs={{1,0},{2,1},{3,2},{4,3},{5,4},{6,5},{7,6},{8,7},{9,8},{10,9},{11,1... | collective-permute-start | bytes 2359304 | tf_op jit(solution)/shard_map/ppermute | solution.py:15
  7.7 1.9 %collective-permute-start.1 = (f32[128,2,768]{2,1,0:T(2,128)S(1)}, f32[128,2,768]{2,1,0:T(2,128)S(1)}, u32[]{:S(2)}, u32[]{:S(2)}) collective-permute-start(f32[128,2,768]{2,1,0:T(2,128)S(1)} %get-tuple-element.15), channel_id=1, source_target_pairs={{0,1},{1,2},{2,3},{3,4},{4,5},{5,6},{6,7},{7,8},{8,9},{9,10},{10,1... | collective-permute-start | bytes 2359304 | tf_op jit(solution)/shard_map/ppermute | solution.py:14
  9.6 0.2 fusion.24
  9.8 0.2 fusion.22
  10.0 0.9 fusion.25
  10.9 0.9 fusion.23
  11.8 5.3 %collective-permute-done = f32[128,2,768]{2,1,0:T(2,128)S(1)} collective-permute-done((f32[128,2,768]{2,1,0:T(2,128)S(1)}, f32[128,2,768]{2,1,0:T(2,128)S(1)}, u32[]{:S(2)}, u32[]{:S(2)}) %collective-permute-start) | collective-permute-done | bytes 786464 | tf_op jit(solution)/shard_map/ppermute | solution.py:15
  17.2 5.9 %collective-permute-done.1 = f32[128,2,768]{2,1,0:T(2,128)S(1)} collective-permute-done((f32[128,2,768]{2,1,0:T(2,128)S(1)}, f32[128,2,768]{2,1,0:T(2,128)S(1)}, u32[]{:S(2)}, u32[]{:S(2)}) %collective-permute-start.1) | collective-permute-done | bytes 786464 | tf_op jit(solution)/shard_map/ppermute | solution.py:14
  23.1 4.9 %fusion.5 = f32[128,4,768]{2,1,0:T(4,128)S(1)} fusion(f32[128,2,768]{2,1,0:T(2,128)S(1)} %collective-permute-done.1, f32[128,4,768]{2,1,0:T(4,128)S(1)} %get-tuple-element.5, f32[128,2,768]{2,1,0:T(2,128)S(1)} %collective-permute-done, f32[128,4,1]{2,1,0:T(4,128)S(1)} %get-tuple-element.11, f32[128,4,767]{2,1,0:T(4,128)S(1)} %get-tuple-element.13, ...), kind=kLoop, calls=%fused_computation.9 | loop fusion | flops 7471104 | bytes 11010048 | tf_op jit(solution)/shard_map/sub | solution.py:52
  28.0 1.7 %fusion.16 = f32[128,128]{0,1:T(8,128)S(1)} fusion(f32[128,4,768]{2,1,0:T(4,128)S(1)} %fusion.5), kind=kOutput, calls=%fused_computation.25 | convolution fusion | flops 603996160 | bytes 1638400 | tf_op jit(solution)/shard_map/dot_general | solution.py:55
  29.7 1.9 %collective-permute-start.2 = (f32[128,128]{0,1:T(8,128)S(1)}, f32[128,128]{0,1:T(8,128)S(1)}, u32[]{:S(2)}, u32[]{:S(2)}) collective-permute-start(f32[128,128]{0,1:T(8,128)S(1)} %fusion.16), channel_id=1, source_target_pairs={{0,1},{1,0},{2,3},{3,2},{4,5},{5,4},{6,7},{7,6},{8,9},{9,8},{10,11... | collective-permute-start | bytes 196616 | tf_op jit(solution)/shard_map/ppermute | solution.py:25
  31.6 1.2 collective-permute-done.2
  32.8 1.9 %collective-permute-start.3 = (f32[128,128]{0,1:T(8,128)S(1)}, f32[128,128]{0,1:T(8,128)S(1)}, u32[]{:S(2)}, u32[]{:S(2)}) collective-permute-start(f32[128,128]{0,1:T(8,128)S(1)} %add.38), channel_id=1, source_target_pairs={{0,2},{1,3},{2,0},{3,1},{4,6},{5,7},{6,4},{7,5},{8,10},{9,11},{10,... | collective-permute-start | bytes 196616 | tf_op jit(solution)/shard_map/ppermute | solution.py:25
  34.8 4.2 %collective-permute-done.3 = f32[128,128]{0,1:T(8,128)S(1)} collective-permute-done((f32[128,128]{0,1:T(8,128)S(1)}, f32[128,128]{0,1:T(8,128)S(1)}, u32[]{:S(2)}, u32[]{:S(2)}) %collective-permute-start.3) | collective-permute-done | bytes 65568 | tf_op jit(solution)/shard_map/ppermute | solution.py:25
  39.0 1.9 %collective-permute-start.4 = (f32[128,128]{0,1:T(8,128)S(1)}, f32[128,128]{0,1:T(8,128)S(1)}, u32[]{:S(2)}, u32[]{:S(2)}) collective-permute-start(f32[128,128]{0,1:T(8,128)S(1)} %add.39), channel_id=1, source_target_pairs={{0,4},{1,5},{2,6},{3,7},{4,0},{5,1},{6,2},{7,3},{8,12},{9,13},{10,... | collective-permute-start | bytes 196616 | tf_op jit(solution)/shard_map/ppermute | solution.py:25
  40.9 5.7 %collective-permute-done.4 = f32[128,128]{0,1:T(8,128)S(1)} collective-permute-done((f32[128,128]{0,1:T(8,128)S(1)}, f32[128,128]{0,1:T(8,128)S(1)}, u32[]{:S(2)}, u32[]{:S(2)}) %collective-permute-start.4) | collective-permute-done | bytes 65568 | tf_op jit(solution)/shard_map/ppermute | solution.py:25
  46.7 17.2 %collective-permute-start.5 = (f32[128,128]{0,1:T(8,128)S(1)}, f32[128,128]{0,1:T(8,128)S(1)}, u32[]{:S(2)}, u32[]{:S(2)}) collective-permute-start(f32[128,128]{0,1:T(8,128)S(1)} %add.40), channel_id=1, source_target_pairs={{0,8},{1,9},{2,10},{3,11},{4,12},{5,13},{6,14},{7,15},{8,0},{9,1},... | collective-permute-start | bytes 196616 | tf_op jit(solution)/shard_map/ppermute | solution.py:25
  63.9 2.2 %collective-permute-done.5 = f32[128,128]{0,1:T(8,128)S(1)} collective-permute-done((f32[128,128]{0,1:T(8,128)S(1)}, f32[128,128]{0,1:T(8,128)S(1)}, u32[]{:S(2)}, u32[]{:S(2)}) %collective-permute-start.5) | collective-permute-done | bytes 65568 | tf_op jit(solution)/shard_map/ppermute | solution.py:25
  66.1 1.9 %collective-permute-start.6 = (f32[128,128]{0,1:T(8,128)S(1)}, f32[128,128]{0,1:T(8,128)S(1)}, u32[]{:S(2)}, u32[]{:S(2)}) collective-permute-start(f32[128,128]{0,1:T(8,128)S(1)} %add.41), channel_id=1, source_target_pairs={{0,16},{1,17},{2,18},{3,19},{4,20},{5,21},{6,22},{7,23},{8,24},{9,... | collective-permute-start | bytes 196616 | tf_op jit(solution)/shard_map/ppermute | solution.py:25
  68.0 5.7 %collective-permute-done.6 = f32[128,128]{0,1:T(8,128)S(1)} collective-permute-done((f32[128,128]{0,1:T(8,128)S(1)}, f32[128,128]{0,1:T(8,128)S(1)}, u32[]{:S(2)}, u32[]{:S(2)}) %collective-permute-start.6) | collective-permute-done | bytes 65568 | tf_op jit(solution)/shard_map/ppermute | solution.py:25
  73.8 1.9 %collective-permute-start.7 = (f32[128,128]{0,1:T(8,128)S(1)}, f32[128,128]{0,1:T(8,128)S(1)}, u32[]{:S(2)}, u32[]{:S(2)}) collective-permute-start(f32[128,128]{0,1:T(8,128)S(1)} %add.42), channel_id=1, source_target_pairs={{0,32},{1,33},{2,34},{3,35},{4,36},{5,37},{6,38},{7,39},{8,40},{9,... | collective-permute-start | bytes 196616 | tf_op jit(solution)/shard_map/ppermute | solution.py:25
  75.7 4.2 %collective-permute-done.7 = f32[128,128]{0,1:T(8,128)S(1)} collective-permute-done((f32[128,128]{0,1:T(8,128)S(1)}, f32[128,128]{0,1:T(8,128)S(1)}, u32[]{:S(2)}, u32[]{:S(2)}) %collective-permute-start.7) | collective-permute-done | bytes 65568 | tf_op jit(solution)/shard_map/ppermute | solution.py:25
  80.0 1.9 %collective-permute-start.8 = (f32[128,128]{0,1:T(8,128)S(1)}, f32[128,128]{0,1:T(8,128)S(1)}, u32[]{:S(2)}, u32[]{:S(2)}) collective-permute-start(f32[128,128]{0,1:T(8,128)S(1)} %add.43), channel_id=1, source_target_pairs={{0,64},{1,65},{2,66},{3,67},{4,68},{5,69},{6,70},{7,71},{8,72},{9,... | collective-permute-start | bytes 196616 | tf_op jit(solution)/shard_map/ppermute | solution.py:25
  81.9 5.8 %collective-permute-done.8 = f32[128,128]{0,1:T(8,128)S(1)} collective-permute-done((f32[128,128]{0,1:T(8,128)S(1)}, f32[128,128]{0,1:T(8,128)S(1)}, u32[]{:S(2)}, u32[]{:S(2)}) %collective-permute-start.8) | collective-permute-done | bytes 65568 | tf_op jit(solution)/shard_map/ppermute | solution.py:25
  87.7 1.9 %collective-permute-start.9 = (f32[128,128]{0,1:T(8,128)S(1)}, f32[128,128]{0,1:T(8,128)S(1)}, u32[]{:S(2)}, u32[]{:S(2)}) collective-permute-start(f32[128,128]{0,1:T(8,128)S(1)} %add.44), channel_id=1, source_target_pairs={{0,128},{1,129},{2,130},{3,131},{4,132},{5,133},{6,134},{7,135},{8... | collective-permute-start | bytes 196616 | tf_op jit(solution)/shard_map/ppermute | solution.py:25
  89.6 9.7 %collective-permute-done.9 = f32[128,128]{0,1:T(8,128)S(1)} collective-permute-done((f32[128,128]{0,1:T(8,128)S(1)}, f32[128,128]{0,1:T(8,128)S(1)}, u32[]{:S(2)}, u32[]{:S(2)}) %collective-permute-start.9) | collective-permute-done | bytes 65568 | tf_op jit(solution)/shard_map/ppermute | solution.py:25
  99.3 8.7 %collective-permute-start.10 = (f32[128,128]{0,1:T(8,128)S(1)}, f32[128,128]{0,1:T(8,128)S(1)}, u32[]{:S(2)}, u32[]{:S(2)}) collective-permute-start(f32[128,128]{0,1:T(8,128)S(1)} %add.45), channel_id=1, source_target_pairs={{0,256},{1,257},{2,258},{3,259},{4,260},{5,261},{6,262},{7,263},{8... | collective-permute-start | bytes 196616 | tf_op jit(solution)/shard_map/ppermute | solution.py:25
  108.0 0.3 copy.12
  108.3 0.5 copy.7
  108.8 5.9 %collective-permute-done.10 = f32[128,128]{0,1:T(8,128)S(1)} collective-permute-done((f32[128,128]{0,1:T(8,128)S(1)}, f32[128,128]{0,1:T(8,128)S(1)}, u32[]{:S(2)}, u32[]{:S(2)}) %collective-permute-start.10) | collective-permute-done | bytes 65568 | tf_op jit(solution)/shard_map/ppermute | solution.py:25
  114.7 0.1 copy.6
  114.8 11.7 %cholesky.17 = f32[128,128]{1,0:T(8,128)S(1)} custom-call(f32[128,128]{1,0:T(8,128)S(1)} %fusion.20), custom_call_target="Cholesky" | custom-call | tf_op jit(solution)/shard_map/jit(cholesky)/cholesky | solution.py:64
  126.5 0.6 compare_reduce_fusion
  127.2 0.7 fusion.21
  127.8 9.8 %custom-call.6 = f32[1,128,128]{1,2,0:T(8,128)S(1)} custom-call(f32[1,128,128]{2,1,0:T(8,128)S(1)} %get-tuple-element.17), custom_call_target="InvertDiagBlocksLowerTriangular" | custom-call | tf_op jit(solution)/shard_map/triangular_solve | solution.py:66
  137.7 0.2 convolution_bitcast_fusion
  137.9 1.5 %fusion.27 = f32[128,4,768]{2,0,1:T(8,128)S(1)} fusion(f32[128,128,1]{1,0,2:T(8,128)S(1)} %convolution_bitcast_fusion, f32[4,768,128]{2,1,0:T(8,128)S(1)} %bitcast.29), kind=kOutput, calls=%fused_computation.41 | convolution fusion | flops 603979776 | bytes 3211264 | tf_op jit(solution)/shard_map/dot_general | solution.py:67
  139.4 2.2 %copy.8 = f32[128,4,768]{2,1,0:T(4,128)} copy(f32[128,4,768]{2,0,1:T(8,128)S(1)} %fusion.27) | data formatting | bytes 3145728
  141.6 0.7 copy.9
  (11 shorter events, 0.1 us)
Async XLA Ops:
  3.7 13.5 %collective-permute-start = (f32[128,2,768]{2,1,0:T(2,128)S(1)}, f32[128,2,768]{2,1,0:T(2,128)S(1)}, u32[]{:S(2)}, u32[]{:S(2)}) collective-permute-start(f32[128,2,768]{2,1,0:T(2,128)S(1)} %get-tuple-element.14), channel_id=1, source_target_pairs={{1,0},{2,1},{3,2},{4,3},{5,4},{6,5},{7,6},{8,7},{9,8},{10,9},{11,1... | collective-permute-start | bytes 2359304 | tf_op jit(solution)/shard_map/ppermute | solution.py:15
  7.7 15.4 %collective-permute-start.1 = (f32[128,2,768]{2,1,0:T(2,128)S(1)}, f32[128,2,768]{2,1,0:T(2,128)S(1)}, u32[]{:S(2)}, u32[]{:S(2)}) collective-permute-start(f32[128,2,768]{2,1,0:T(2,128)S(1)} %get-tuple-element.15), channel_id=1, source_target_pairs={{0,1},{1,2},{2,3},{3,4},{4,5},{5,6},{6,7},{7,8},{8,9},{9,10},{10,1... | collective-permute-start | bytes 2359304 | tf_op jit(solution)/shard_map/ppermute | solution.py:14
  29.7 3.1 %collective-permute-start.2 = (f32[128,128]{0,1:T(8,128)S(1)}, f32[128,128]{0,1:T(8,128)S(1)}, u32[]{:S(2)}, u32[]{:S(2)}) collective-permute-start(f32[128,128]{0,1:T(8,128)S(1)} %fusion.16), channel_id=1, source_target_pairs={{0,1},{1,0},{2,3},{3,2},{4,5},{5,4},{6,7},{7,6},{8,9},{9,8},{10,11... | collective-permute-start | bytes 196616 | tf_op jit(solution)/shard_map/ppermute | solution.py:25
  32.8 6.2 %collective-permute-start.3 = (f32[128,128]{0,1:T(8,128)S(1)}, f32[128,128]{0,1:T(8,128)S(1)}, u32[]{:S(2)}, u32[]{:S(2)}) collective-permute-start(f32[128,128]{0,1:T(8,128)S(1)} %add.38), channel_id=1, source_target_pairs={{0,2},{1,3},{2,0},{3,1},{4,6},{5,7},{6,4},{7,5},{8,10},{9,11},{10,... | collective-permute-start | bytes 196616 | tf_op jit(solution)/shard_map/ppermute | solution.py:25
  39.0 7.7 %collective-permute-start.4 = (f32[128,128]{0,1:T(8,128)S(1)}, f32[128,128]{0,1:T(8,128)S(1)}, u32[]{:S(2)}, u32[]{:S(2)}) collective-permute-start(f32[128,128]{0,1:T(8,128)S(1)} %add.39), channel_id=1, source_target_pairs={{0,4},{1,5},{2,6},{3,7},{4,0},{5,1},{6,2},{7,3},{8,12},{9,13},{10,... | collective-permute-start | bytes 196616 | tf_op jit(solution)/shard_map/ppermute | solution.py:25
  46.7 19.4 %collective-permute-start.5 = (f32[128,128]{0,1:T(8,128)S(1)}, f32[128,128]{0,1:T(8,128)S(1)}, u32[]{:S(2)}, u32[]{:S(2)}) collective-permute-start(f32[128,128]{0,1:T(8,128)S(1)} %add.40), channel_id=1, source_target_pairs={{0,8},{1,9},{2,10},{3,11},{4,12},{5,13},{6,14},{7,15},{8,0},{9,1},... | collective-permute-start | bytes 196616 | tf_op jit(solution)/shard_map/ppermute | solution.py:25
  66.1 7.7 %collective-permute-start.6 = (f32[128,128]{0,1:T(8,128)S(1)}, f32[128,128]{0,1:T(8,128)S(1)}, u32[]{:S(2)}, u32[]{:S(2)}) collective-permute-start(f32[128,128]{0,1:T(8,128)S(1)} %add.41), channel_id=1, source_target_pairs={{0,16},{1,17},{2,18},{3,19},{4,20},{5,21},{6,22},{7,23},{8,24},{9,... | collective-permute-start | bytes 196616 | tf_op jit(solution)/shard_map/ppermute | solution.py:25
  73.8 6.2 %collective-permute-start.7 = (f32[128,128]{0,1:T(8,128)S(1)}, f32[128,128]{0,1:T(8,128)S(1)}, u32[]{:S(2)}, u32[]{:S(2)}) collective-permute-start(f32[128,128]{0,1:T(8,128)S(1)} %add.42), channel_id=1, source_target_pairs={{0,32},{1,33},{2,34},{3,35},{4,36},{5,37},{6,38},{7,39},{8,40},{9,... | collective-permute-start | bytes 196616 | tf_op jit(solution)/shard_map/ppermute | solution.py:25
  80.0 7.7 %collective-permute-start.8 = (f32[128,128]{0,1:T(8,128)S(1)}, f32[128,128]{0,1:T(8,128)S(1)}, u32[]{:S(2)}, u32[]{:S(2)}) collective-permute-start(f32[128,128]{0,1:T(8,128)S(1)} %add.43), channel_id=1, source_target_pairs={{0,64},{1,65},{2,66},{3,67},{4,68},{5,69},{6,70},{7,71},{8,72},{9,... | collective-permute-start | bytes 196616 | tf_op jit(solution)/shard_map/ppermute | solution.py:25
  87.7 11.6 %collective-permute-start.9 = (f32[128,128]{0,1:T(8,128)S(1)}, f32[128,128]{0,1:T(8,128)S(1)}, u32[]{:S(2)}, u32[]{:S(2)}) collective-permute-start(f32[128,128]{0,1:T(8,128)S(1)} %add.44), channel_id=1, source_target_pairs={{0,128},{1,129},{2,130},{3,131},{4,132},{5,133},{6,134},{7,135},{8... | collective-permute-start | bytes 196616 | tf_op jit(solution)/shard_map/ppermute | solution.py:25
  99.3 15.3 %collective-permute-start.10 = (f32[128,128]{0,1:T(8,128)S(1)}, f32[128,128]{0,1:T(8,128)S(1)}, u32[]{:S(2)}, u32[]{:S(2)}) collective-permute-start(f32[128,128]{0,1:T(8,128)S(1)} %add.45), channel_id=1, source_target_pairs={{0,256},{1,257},{2,258},{3,259},{4,260},{5,261},{6,262},{7,263},{8... | collective-permute-start | bytes 196616 | tf_op jit(solution)/shard_map/ppermute | solution.py:25

commit v2 on v1

v2 whole, which is shorter than its diff:
```python
import jax
import jax.numpy as jnp
from jax import lax
from jax.sharding import Mesh
from jax.sharding import PartitionSpec as P

AXES = ("zh", "zl", "y", "x", "core")


def ring_index(shape):
    size = 1
    for s in shape:
        size *= s
    return size


def extended(array, axes, size, dim, width):
    length = array.shape[dim]
    up = [(i, (i + 1) % size) for i in range(size)]
    down = [(j, i) for i, j in up]
    last = lax.slice_in_dim(array, length - width, length, axis=dim)
    initial = lax.slice_in_dim(array, 0, width, axis=dim)
    before = lax.ppermute(last, axes, up)
    after = lax.ppermute(initial, axes, down)
    return jnp.concatenate([before, array, after], axis=dim)


def tree_sum(values):
    while len(values) > 1:
        values = [values[i] + values[i + 1] for i in range(0, len(values), 2)]
    return values[0]


def gather_sum(value, axes, count):
    stacked = jnp.broadcast_to(value[None], (count,) + value.shape)
    gathered = lax.all_to_all(stacked, axes, 0, 0, tiled=True)
    return tree_sum([gathered[m] for m in range(count)])


def butterfly_sum(value, axis, size):
    bit = 1
    while bit < size:
        pairs = [(i, i ^ bit) for i in range(size)]
        value = value + lax.ppermute(value, axis, pairs)
        bit *= 2
    return value


def along_second(field):
    return (
        8.0 * (jnp.roll(field, -1, 2) - jnp.roll(field, 1, 2))
        - (jnp.roll(field, -2, 2) - jnp.roll(field, 2, 2))
    ) / 12.0


def stencil_rows(padded, row_count):
    return 8.0 * (padded[:, 3 : row_count + 3] - padded[:, 1 : row_count + 1]) - (
        padded[:, 4 : row_count + 4] - padded[:, 0:row_count]
    )


def make_local(sizes):
    total = ring_index(sizes.values())

    def local(velocity):
        snap_count = velocity.shape[1]
        row_count = velocity.shape[2]
        col_count = velocity.shape[3]
        total_cells = row_count * total * col_count
        comp_u = velocity[0]
        comp_v = velocity[1]
        padded = extended(comp_v, AXES, total, 1, 2)
        v_first = stencil_rows(padded, row_count) / 12.0
        vorticity = v_first - along_second(comp_u)
        flattened = vorticity.reshape(snap_count, row_count * col_count)
        local_gram = (
            jnp.dot(
                flattened,
                flattened.T,
                precision=lax.Precision.HIGHEST,
                preferred_element_type=jnp.float32,
            )
            / total_cells
        )
        gram = gather_sum(local_gram, ("x", "core"), sizes["x"] * sizes["core"])
        gram = gather_sum(gram, ("y",), sizes["y"])
        gram = gather_sum(gram, ("zl",), sizes["zl"])
        gram = butterfly_sum(gram, "zh", sizes["zh"])
        lower = jnp.linalg.cholesky(gram)
        identity = jnp.eye(snap_count, dtype=jnp.float32)
        inverse_lower = lax.linalg.triangular_solve(lower, identity, left_side=True, lower=True)
        spatial_modes = jnp.dot(
            inverse_lower,
            flattened,
            precision=lax.Precision.HIGHEST,
            preferred_element_type=jnp.float32,
        )
        return (spatial_modes.reshape(snap_count, row_count, col_count), lower.T)

    return local


def solution(mesh):
    devices = mesh.devices.reshape(-1)
    count = devices.shape[0]
    core = 2
    x_size = 4 if count % (core * 4) == 0 else 1
    y_size = 4 if count % (core * x_size * 4) == 0 else 1
    rest = count // (core * x_size * y_size)
    zl = 4 if rest % 4 == 0 else rest
    zh = rest // zl
    sizes = {"zh": zh, "zl": zl, "y": y_size, "x": x_size, "core": core}
    view = Mesh(devices.reshape(zh, zl, y_size, x_size, core), AXES)
    return jax.shard_map(
        make_local(sizes),
        mesh=view,
        in_specs=(P(None, None, AXES, None),),
        out_specs=(P(None, AXES, None), P()),
        check_vma=False,
    )
```

time: 143 us -> 132 us (0.923)
  the two profiles are of different devices: /device:TPU:8 before, /device:TPU:2 now
where the time goes in v2:
time: 132 us
  blocking collectives  45.9 us (35%)
  waiting for transfers between devices  32 us (24%)
  other arithmetic  27.8 us (21%)
  starting transfers between devices  13 us (10%)
  local copies, waits for them, and re-layouts  9.11 us (7%)
  matrix products  3.43 us (3%)
    all_to_all x3, blocking collectives, gather_sum(): gathered = lax.all_to_all(stacked, axes, 0, 0, tiled=True)  45.9 us
    ppermute x2, waiting for transfers between devices, butterfly_sum(): value = value + lax.ppermute(value, axis, pairs)  19 us
    another operation x3, other arithmetic, local(): lower = jnp.linalg.cholesky(gram)  12.4 us
    another operation x1, other arithmetic, local(): lax.linalg.triangular_solve(lower, identity, left_side=True, lower=True)  9.81 us
    ppermute x2, starting transfers between devices, butterfly_sum(): value = value + lax.ppermute(value, axis, pairs)  8.64 us
    ppermute x1, waiting for transfers between devices, extended(): before = lax.ppermute(last, axes, up)  8.1 us
    sub x1, other arithmetic, local(): vorticity = v_first - along_second(comp_u)  4.88 us
    ppermute x1, waiting for transfers between devices, extended(): after = lax.ppermute(initial, axes, down)  4.85 us
  transfers between devices with their start and end apart: 4, of which 4 were waited for; matrix products, arithmetic and copies ran while one was open for 2% of the time, Pallas kernels for 0%

profile of v2, /device:TPU:2, one launch (start us, length us, event | category | flops | bytes accessed | tf_op | source)
XLA Modules:
  0.0 132.0 jit_solution(11911654894231552177)
XLA Ops:
  0.6 2.4 %slice_bitcast_fusion = (f32[128,4,768]{2,1,0:T(4,128)S(1)}, f32[128,4,768]{2,1,0:T(4,128)S(1)}) fusion(f32[2,128,4,768]{3,2,1,0:T(4,128)} %param.1), kind=kLoop, calls=%fused_computation.21 | loop fusion | bytes 6291456 | tf_op jit(solution)/shard_map/squeeze | solution.py:70
  3.1 0.6 fusion.34
  3.7 1.9 %collective-permute-start = (f32[128,2,768]{2,1,0:T(2,128)S(1)}, f32[128,2,768]{2,1,0:T(2,128)S(1)}, u32[]{:S(2)}, u32[]{:S(2)}) collective-permute-start(f32[128,2,768]{2,1,0:T(2,128)S(1)} %get-tuple-element.14), channel_id=1, source_target_pairs={{1,0},{2,1},{3,2},{4,3},{5,4},{6,5},{7,6},{8,7},{9,8},{10,9},{11,1... | collective-permute-start | bytes 2359304 | tf_op jit(solution)/shard_map/ppermute | solution.py:24
  5.6 2.4 %collective-permute-start.1 = (f32[128,2,768]{2,1,0:T(2,128)S(1)}, f32[128,2,768]{2,1,0:T(2,128)S(1)}, u32[]{:S(2)}, u32[]{:S(2)}) collective-permute-start(f32[128,2,768]{2,1,0:T(2,128)S(1)} %get-tuple-element.15), channel_id=1, source_target_pairs={{0,1},{1,2},{2,3},{3,4},{4,5},{5,6},{6,7},{7,8},{8,9},{9,10},{10,1... | collective-permute-start | bytes 2359304 | tf_op jit(solution)/shard_map/ppermute | solution.py:23
  8.0 0.2 fusion.32
  8.2 0.2 fusion.30
  8.4 0.9 fusion.33
  9.3 0.9 fusion.31
  10.2 4.8 %collective-permute-done = f32[128,2,768]{2,1,0:T(2,128)S(1)} collective-permute-done((f32[128,2,768]{2,1,0:T(2,128)S(1)}, f32[128,2,768]{2,1,0:T(2,128)S(1)}, u32[]{:S(2)}, u32[]{:S(2)}) %collective-permute-start) | collective-permute-done | bytes 786464 | tf_op jit(solution)/shard_map/ppermute | solution.py:24
  15.1 8.1 %collective-permute-done.1 = f32[128,2,768]{2,1,0:T(2,128)S(1)} collective-permute-done((f32[128,2,768]{2,1,0:T(2,128)S(1)}, f32[128,2,768]{2,1,0:T(2,128)S(1)}, u32[]{:S(2)}, u32[]{:S(2)}) %collective-permute-start.1) | collective-permute-done | bytes 786464 | tf_op jit(solution)/shard_map/ppermute | solution.py:23
  23.2 4.9 %fusion.5 = f32[128,4,768]{2,1,0:T(4,128)S(1)} fusion(f32[128,2,768]{2,1,0:T(2,128)S(1)} %collective-permute-done.1, f32[128,4,768]{2,1,0:T(4,128)S(1)} %get-tuple-element.5, f32[128,2,768]{2,1,0:T(2,128)S(1)} %collective-permute-done, f32[128,4,1]{2,1,0:T(4,128)S(1)} %get-tuple-element.11, f32[128,4,767]{2,1,0:T(4,128)S(1)} %get-tuple-element.13, ...), kind=kLoop, calls=%fused_computation.9 | loop fusion | flops 7471104 | bytes 11010048 | tf_op jit(solution)/shard_map/sub | solution.py:74
  28.1 1.7 %fusion.16 = f32[128,128]{1,0:T(8,128)S(1)} fusion(f32[128,4,768]{2,1,0:T(4,128)S(1)} %fusion.5), kind=kOutput, calls=%fused_computation.25 | convolution fusion | flops 603996160 | bytes 1638400 | tf_op jit(solution)/shard_map/dot_general | solution.py:77
  29.8 0.1 copy.5
  29.9 26.6 %all_to_all.15 = f32[8,128,128]{1,2,0:T(8,128)S(1)} all-to-all(f32[8,128,128]{1,2,0:T(8,128)S(1)} %broadcast_in_dim.11), channel_id=1, replica_groups=mesh['zh'=4,'zl'=4,'y'=4,'x'=4,'core'=2] {'x','core'}, dimensions={0} | all-to-all | bytes 1048576 | tf_op jit(solution)/shard_map/all_to_all | solution.py:36
  56.6 9.1 %all_to_all.16 = f32[4,128,128]{1,2,0:T(8,128)S(1)} all-to-all(f32[4,128,128]{1,2,0:T(8,128)S(1)} %broadcast_in_dim.26), channel_id=1, replica_groups=mesh['zh'=4,'zl'=4,'y'=4,'x'=4,'core'=2] {'y'}, dimensions={0} | all-to-all | bytes 524288 | tf_op jit(solution)/shard_map/all_to_all | solution.py:36
  65.7 10.2 %all_to_all.17 = f32[4,128,128]{1,2,0:T(8,128)S(1)} all-to-all(f32[4,128,128]{1,2,0:T(8,128)S(1)} %broadcast_in_dim.28), channel_id=1, replica_groups=mesh['zh'=4,'zl'=4,'y'=4,'x'=4,'core'=2] {'zl'}, dimensions={0} | all-to-all | bytes 524288 | tf_op jit(solution)/shard_map/all_to_all | solution.py:36
  75.9 1.9 %collective-permute-start.2 = (f32[128,128]{0,1:T(8,128)S(1)}, f32[128,128]{0,1:T(8,128)S(1)}, u32[]{:S(2)}, u32[]{:S(2)}) collective-permute-start(f32[128,128]{0,1:T(8,128)S(1)} %fusion.20), channel_id=1, source_target_pairs={{0,128},{128,0},{256,384},{384,256},{1,129},{129,1},{257,385},{385... | collective-permute-start | bytes 196616 | tf_op jit(solution)/shard_map/ppermute | solution.py:44
  77.8 9.7 %collective-permute-done.2 = f32[128,128]{0,1:T(8,128)S(1)} collective-permute-done((f32[128,128]{0,1:T(8,128)S(1)}, f32[128,128]{0,1:T(8,128)S(1)}, u32[]{:S(2)}, u32[]{:S(2)}) %collective-permute-start.2) | collective-permute-done | bytes 65568 | tf_op jit(solution)/shard_map/ppermute | solution.py:44
  87.6 6.7 %collective-permute-start.3 = (f32[128,128]{0,1:T(8,128)S(1)}, f32[128,128]{0,1:T(8,128)S(1)}, u32[]{:S(2)}, u32[]{:S(2)}) collective-permute-start(f32[128,128]{0,1:T(8,128)S(1)} %fusion.38), channel_id=1, source_target_pairs={{0,256},{128,384},{256,0},{384,128},{1,257},{129,385},{257,1},{385... | collective-permute-start | bytes 196616 | tf_op jit(solution)/shard_map/ppermute | solution.py:44
  94.3 0.3 copy.10
  94.6 0.5 copy.7
  95.1 9.3 %collective-permute-done.3 = f32[128,128]{0,1:T(8,128)S(1)} collective-permute-done((f32[128,128]{0,1:T(8,128)S(1)}, f32[128,128]{0,1:T(8,128)S(1)}, u32[]{:S(2)}, u32[]{:S(2)}) %collective-permute-start.3) | collective-permute-done | bytes 65568 | tf_op jit(solution)/shard_map/ppermute | solution.py:44
  104.4 0.1 copy.6
  104.5 11.7 %cholesky.17 = f32[128,128]{1,0:T(8,128)S(1)} custom-call(f32[128,128]{1,0:T(8,128)S(1)} %fusion.28), custom_call_target="Cholesky" | custom-call | tf_op jit(solution)/shard_map/jit(cholesky)/cholesky | solution.py:89
  116.2 0.6 compare_reduce_fusion
  116.9 0.7 fusion.29
  117.5 9.8 %custom-call.6 = f32[1,128,128]{1,2,0:T(8,128)S(1)} custom-call(f32[1,128,128]{2,1,0:T(8,128)S(1)} %get-tuple-element.17), custom_call_target="InvertDiagBlocksLowerTriangular" | custom-call | tf_op jit(solution)/shard_map/triangular_solve | solution.py:91
  127.3 0.2 convolution_bitcast_fusion
  127.6 1.5 %fusion.35 = f32[128,4,768]{2,0,1:T(8,128)S(1)} fusion(f32[128,128,1]{1,0,2:T(8,128)S(1)} %convolution_bitcast_fusion, f32[4,768,128]{2,1,0:T(8,128)S(1)} %bitcast.37), kind=kOutput, calls=%fused_computation.57 | convolution fusion | flops 603979776 | bytes 3211264 | tf_op jit(solution)/shard_map/dot_general | solution.py:92
  129.1 2.2 %copy.8 = f32[128,4,768]{2,1,0:T(4,128)} copy(f32[128,4,768]{2,0,1:T(8,128)S(1)} %fusion.35) | data formatting | bytes 3145728
  131.3 0.7 copy.9
  (10 shorter events, 0.2 us)
Async XLA Ops:
  3.7 11.4 %collective-permute-start = (f32[128,2,768]{2,1,0:T(2,128)S(1)}, f32[128,2,768]{2,1,0:T(2,128)S(1)}, u32[]{:S(2)}, u32[]{:S(2)}) collective-permute-start(f32[128,2,768]{2,1,0:T(2,128)S(1)} %get-tuple-element.14), channel_id=1, source_target_pairs={{1,0},{2,1},{3,2},{4,3},{5,4},{6,5},{7,6},{8,7},{9,8},{10,9},{11,1... | collective-permute-start | bytes 2359304 | tf_op jit(solution)/shard_map/ppermute | solution.py:24
  5.6 17.6 %collective-permute-start.1 = (f32[128,2,768]{2,1,0:T(2,128)S(1)}, f32[128,2,768]{2,1,0:T(2,128)S(1)}, u32[]{:S(2)}, u32[]{:S(2)}) collective-permute-start(f32[128,2,768]{2,1,0:T(2,128)S(1)} %get-tuple-element.15), channel_id=1, source_target_pairs={{0,1},{1,2},{2,3},{3,4},{4,5},{5,6},{6,7},{7,8},{8,9},{9,10},{10,1... | collective-permute-start | bytes 2359304 | tf_op jit(solution)/shard_map/ppermute | solution.py:23
  75.9 11.7 %collective-permute-start.2 = (f32[128,128]{0,1:T(8,128)S(1)}, f32[128,128]{0,1:T(8,128)S(1)}, u32[]{:S(2)}, u32[]{:S(2)}) collective-permute-start(f32[128,128]{0,1:T(8,128)S(1)} %fusion.20), channel_id=1, source_target_pairs={{0,128},{128,0},{256,384},{384,256},{1,129},{129,1},{257,385},{385... | collective-permute-start | bytes 196616 | tf_op jit(solution)/shard_map/ppermute | solution.py:44
  87.6 16.7 %collective-permute-start.3 = (f32[128,128]{0,1:T(8,128)S(1)}, f32[128,128]{0,1:T(8,128)S(1)}, u32[]{:S(2)}, u32[]{:S(2)}) collective-permute-start(f32[128,128]{0,1:T(8,128)S(1)} %fusion.38), channel_id=1, source_target_pairs={{0,256},{128,384},{256,0},{384,128},{1,257},{129,385},{257,1},{385... | collective-permute-start | bytes 196616 | tf_op jit(solution)/shard_map/ppermute | solution.py:44

commit v3 on v2

--- a/solution.py
+++ b/solution.py
@@ -1,6 +1,8 @@
 import jax
 import jax.numpy as jnp
 from jax import lax
+from jax.experimental import pallas as pl
+from jax.experimental.pallas import tpu as pltpu
 from jax.sharding import Mesh
 from jax.sharding import PartitionSpec as P
 
@@ -23,6 +25,49 @@
     before = lax.ppermute(last, axes, up)
     after = lax.ppermute(initial, axes, down)
     return jnp.concatenate([before, array, after], axis=dim)
+
+
+def factor_kernel(gram_ref, upper_ref, inverse_ref, rest_ref, ops_ref):
+    size = gram_ref.shape[0]
+    rows = lax.broadcasted_iota(jnp.int32, (size, size), 0)
+    cols = lax.broadcasted_iota(jnp.int32, (size, size), 1)
+    lane = lax.broadcasted_iota(jnp.int32, (1, size), 1)
+    sublane = lax.broadcasted_iota(jnp.int32, (size, 1), 0)
+    rest_ref[...] = gram_ref[...]
+    ops_ref[...] = jnp.where(rows == cols, 1.0, 0.0).astype(jnp.float32)
+
+    def step(j, carry):
+        rest = rest_ref[...]
+        row = rest_ref[pl.ds(j, 1), :]
+        ops_row = ops_ref[pl.ds(j, 1), :]
+        pivot = jnp.sum(jnp.where(lane == j, row, 0.0), axis=1, keepdims=True)
+        root = jnp.sqrt(pivot)
+        factor_row = jnp.where(lane >= j, row / root, 0.0)
+        inverse_row = ops_row / root
+        upper_ref[pl.ds(j, 1), :] = factor_row
+        inverse_ref[pl.ds(j, 1), :] = inverse_row
+        column = jnp.sum(jnp.where(cols == j, rest, 0.0), axis=1, keepdims=True)
+        factor_col = jnp.where(sublane > j, column / root, 0.0)
+        rest_ref[...] = rest - factor_col * factor_row
+        ops_ref[...] = ops_ref[...] - factor_col * inverse_row
+        return carry
+
+    lax.fori_loop(0, size, step, 0)
+
+
+def factor(gram):
+    size = gram.shape[0]
+    vmem = pltpu.VMEM
+    return pl.pallas_call(
+        factor_kernel,
+        out_shape=(
+            jax.ShapeDtypeStruct((size, size), jnp.float32),
+            jax.ShapeDtypeStruct((size, size), jnp.float32),
+        ),
+        in_specs=[pl.BlockSpec(memory_space=vmem)],
+        out_specs=(pl.BlockSpec(memory_space=vmem), pl.BlockSpec(memory_space=vmem)),
+        scratch_shapes=[vmem((size, size), jnp.float32), vmem((size, size), jnp.float32)],
+    )(gram)
 
 
 def tree_sum(values):
@@ -86,16 +131,14 @@
         gram = gather_sum(gram, ("y",), sizes["y"])
         gram = gather_sum(gram, ("zl",), sizes["zl"])
         gram = butterfly_sum(gram, "zh", sizes["zh"])
-        lower = jnp.linalg.cholesky(gram)
-        identity = jnp.eye(snap_count, dtype=jnp.float32)
-        inverse_lower = lax.linalg.triangular_solve(lower, identity, left_side=True, lower=True)
+        upper, inverse_lower = factor(gram)
         spatial_modes = jnp.dot(
             inverse_lower,
             flattened,
             precision=lax.Precision.HIGHEST,
             preferred_element_type=jnp.float32,
         )
-        return (spatial_modes.reshape(snap_count, row_count, col_count), lower.T)
+        return (spatial_modes.reshape(snap_count, row_count, col_count), upper)
 
     return local
 

time: 132 us -> 125 us (0.947)
  other arithmetic: 27.8 us -> 5.6 us
  Pallas kernels: 0 us -> 15.7 us
    another operation x4 -> x0, other arithmetic: 22.2 us -> none  [the longest x3 12.4 us: local(): lower = jnp.linalg.cholesky(gram)]
    pallas_call x0 -> x1, Pallas kernels: none -> 15.7 us  [factor(): pl.pallas_call(factor_kernel, out_shape=(jax.ShapeDtypeStruct((size, size...]
    unnamed x3 -> x2, local copies, waits for them, and re-layouts: 3.16 us -> 2.43 us
where the time goes in v3:
time: 125 us
  blocking collectives  45.9 us (37%)
  waiting for transfers between devices  32.1 us (26%)
  Pallas kernels  15.7 us (13%)
  starting transfers between devices  12.8 us (10%)
  local copies, waits for them, and re-layouts  8.2 us (7%)
  other arithmetic  5.6 us (4%)
  matrix products  4.01 us (3%)
    all_to_all x3, blocking collectives, gather_sum(): gathered = lax.all_to_all(stacked, axes, 0, 0, tiled=True)  45.9 us
    ppermute x2, waiting for transfers between devices, butterfly_sum(): value = value + lax.ppermute(value, axis, pairs)  19.2 us
    pallas_call x1, Pallas kernels, factor(): pl.pallas_call(factor_kernel, out_shape=(jax.ShapeDtypeStruct((size, size...  15.7 us
    ppermute x2, starting transfers between devices, butterfly_sum(): value = value + lax.ppermute(value, axis, pairs)  8.45 us
    ppermute x1, waiting for transfers between devices, extended(): before = lax.ppermute(last, axes, up)  8.1 us
    sub x1, other arithmetic, local(): vorticity = v_first - along_second(comp_u)  4.88 us
    ppermute x1, waiting for transfers between devices, extended(): after = lax.ppermute(initial, axes, down)  4.85 us
  transfers between devices with their start and end apart: 4, of which 4 were waited for; matrix products, arithmetic and copies ran while one was open for 2% of the time, Pallas kernels for 0%

profile of v3, /device:TPU:2, one launch (start us, length us, event | category | flops | bytes accessed | tf_op | source)
XLA Modules:
  0.0 125.0 jit_solution(11187236580170460949)
XLA Ops:
  0.6 2.4 %slice_bitcast_fusion = (f32[128,4,768]{2,1,0:T(4,128)S(1)}, f32[128,4,768]{2,1,0:T(4,128)S(1)}) fusion(f32[2,128,4,768]{3,2,1,0:T(4,128)} %param.1), kind=kLoop, calls=%fused_computation.21 | loop fusion | bytes 6291456 | tf_op jit(solution)/shard_map/squeeze | solution.py:115
  3.1 0.6 fusion.33
  3.7 1.9 %collective-permute-start = (f32[128,2,768]{2,1,0:T(2,128)S(1)}, f32[128,2,768]{2,1,0:T(2,128)S(1)}, u32[]{:S(2)}, u32[]{:S(2)}) collective-permute-start(f32[128,2,768]{2,1,0:T(2,128)S(1)} %get-tuple-element.18), channel_id=1, source_target_pairs={{1,0},{2,1},{3,2},{4,3},{5,4},{6,5},{7,6},{8,7},{9,8},{10,9},{11,1... | collective-permute-start | bytes 2359304 | tf_op jit(solution)/shard_map/ppermute | solution.py:26
  5.6 2.4 %collective-permute-start.1 = (f32[128,2,768]{2,1,0:T(2,128)S(1)}, f32[128,2,768]{2,1,0:T(2,128)S(1)}, u32[]{:S(2)}, u32[]{:S(2)}) collective-permute-start(f32[128,2,768]{2,1,0:T(2,128)S(1)} %get-tuple-element.19), channel_id=1, source_target_pairs={{0,1},{1,2},{2,3},{3,4},{4,5},{5,6},{6,7},{7,8},{8,9},{9,10},{10,1... | collective-permute-start | bytes 2359304 | tf_op jit(solution)/shard_map/ppermute | solution.py:25
  8.0 0.2 fusion.29
  8.2 0.2 fusion.31
  8.4 0.9 fusion.30
  9.3 0.9 fusion.32
  10.2 4.8 %collective-permute-done = f32[128,2,768]{2,1,0:T(2,128)S(1)} collective-permute-done((f32[128,2,768]{2,1,0:T(2,128)S(1)}, f32[128,2,768]{2,1,0:T(2,128)S(1)}, u32[]{:S(2)}, u32[]{:S(2)}) %collective-permute-start) | collective-permute-done | bytes 786464 | tf_op jit(solution)/shard_map/ppermute | solution.py:26
  15.1 8.1 %collective-permute-done.1 = f32[128,2,768]{2,1,0:T(2,128)S(1)} collective-permute-done((f32[128,2,768]{2,1,0:T(2,128)S(1)}, f32[128,2,768]{2,1,0:T(2,128)S(1)}, u32[]{:S(2)}, u32[]{:S(2)}) %collective-permute-start.1) | collective-permute-done | bytes 786464 | tf_op jit(solution)/shard_map/ppermute | solution.py:25
  23.2 4.9 %fusion.5 = f32[128,4,768]{2,1,0:T(4,128)S(1)} fusion(f32[128,2,768]{2,1,0:T(2,128)S(1)} %collective-permute-done.1, f32[128,4,768]{2,1,0:T(4,128)S(1)} %get-tuple-element.9, f32[128,2,768]{2,1,0:T(2,128)S(1)} %collective-permute-done, f32[128,4,1]{2,1,0:T(4,128)S(1)} %get-tuple-element.15, f32[128,4,767]{2,1,0:T(4,128)S(1)} %get-tuple-element.17, ...), kind=kLoop, calls=%fused_computation.9 | loop fusion | flops 7471104 | bytes 11010048 | tf_op jit(solution)/shard_map/sub | solution.py:119
  28.1 1.7 %fusion.16 = f32[128,128]{1,0:T(8,128)S(1)} fusion(f32[128,4,768]{2,1,0:T(4,128)S(1)} %fusion.5), kind=kOutput, calls=%fused_computation.24 | convolution fusion | flops 603996160 | bytes 1638400 | tf_op jit(solution)/shard_map/dot_general | solution.py:122
  29.8 26.6 %all_to_all.15 = f32[8,128,128]{2,1,0:T(8,128)S(1)} all-to-all(f32[8,128,128]{2,1,0:T(8,128)S(1)} %broadcast_in_dim.10), channel_id=1, replica_groups=mesh['zh'=4,'zl'=4,'y'=4,'x'=4,'core'=2] {'x','core'}, dimensions={0} | all-to-all | bytes 1048576 | tf_op jit(solution)/shard_map/all_to_all | solution.py:81
  56.5 9.1 %all_to_all.16 = f32[4,128,128]{2,1,0:T(8,128)S(1)} all-to-all(f32[4,128,128]{2,1,0:T(8,128)S(1)} %broadcast_in_dim.24), channel_id=1, replica_groups=mesh['zh'=4,'zl'=4,'y'=4,'x'=4,'core'=2] {'y'}, dimensions={0} | all-to-all | bytes 524288 | tf_op jit(solution)/shard_map/all_to_all | solution.py:81
  65.6 10.2 %all_to_all.17 = f32[4,128,128]{2,1,0:T(8,128)S(1)} all-to-all(f32[4,128,128]{2,1,0:T(8,128)S(1)} %broadcast_in_dim.26), channel_id=1, replica_groups=mesh['zh'=4,'zl'=4,'y'=4,'x'=4,'core'=2] {'zl'}, dimensions={0} | all-to-all | bytes 524288 | tf_op jit(solution)/shard_map/all_to_all | solution.py:81
  75.8 1.9 %collective-permute-start.2 = (f32[128,128]{1,0:T(8,128)S(1)}, f32[128,128]{1,0:T(8,128)S(1)}, u32[]{:S(2)}, u32[]{:S(2)}) collective-permute-start(f32[128,128]{1,0:T(8,128)S(1)} %fusion.20), channel_id=1, source_target_pairs={{0,128},{128,0},{256,384},{384,256},{1,129},{129,1},{257,385},{385... | collective-permute-start | bytes 196616 | tf_op jit(solution)/shard_map/ppermute | solution.py:89
  77.7 9.7 %collective-permute-done.2 = f32[128,128]{1,0:T(8,128)S(1)} collective-permute-done((f32[128,128]{1,0:T(8,128)S(1)}, f32[128,128]{1,0:T(8,128)S(1)}, u32[]{:S(2)}, u32[]{:S(2)}) %collective-permute-start.2) | collective-permute-done | bytes 65568 | tf_op jit(solution)/shard_map/ppermute | solution.py:89
  87.5 6.5 %collective-permute-start.3 = (f32[128,128]{1,0:T(8,128)S(1)}, f32[128,128]{1,0:T(8,128)S(1)}, u32[]{:S(2)}, u32[]{:S(2)}) collective-permute-start(f32[128,128]{1,0:T(8,128)S(1)} %fusion.35), channel_id=1, source_target_pairs={{0,256},{128,384},{256,0},{384,128},{1,257},{129,385},{257,1},{385... | collective-permute-start | bytes 196616 | tf_op jit(solution)/shard_map/ppermute | solution.py:89
  94.0 0.3 copy.7
  94.3 0.5 copy.5
  94.8 9.4 %collective-permute-done.3 = f32[128,128]{1,0:T(8,128)S(1)} collective-permute-done((f32[128,128]{1,0:T(8,128)S(1)}, f32[128,128]{1,0:T(8,128)S(1)}, u32[]{:S(2)}, u32[]{:S(2)}) %collective-permute-start.3) | collective-permute-done | bytes 65568 | tf_op jit(solution)/shard_map/ppermute | solution.py:89
  104.2 0.6 add.75.gram_ref
  104.9 15.7 %shard_map.30 = (f32[128,128]{1,0:T(8,128)}, f32[128,128]{1,0:T(8,128)}) custom-call(f32[128,128]{1,0:T(8,128)} %add.75.gram_ref), custom_call_target="tpu_custom_call" | custom-call | tf_op jit(solution)/shard_map/pallas_call | solution.py:61
  120.6 2.3 %fusion.27 = f32[128,4,768]{2,0,1:T(8,128)S(1)} fusion(f32[4,768,128]{2,1,0:T(8,128)S(1)} %bitcast.26, f32[128,128]{1,0:T(8,128)} %get-tuple-element.4), kind=kOutput, calls=%fused_computation.41 | convolution fusion | flops 603979776 | bytes 3211264 | tf_op jit(solution)/shard_map/dot_general | solution.py:135
  122.9 2.2 %copy.6 = f32[128,4,768]{2,1,0:T(4,128)} copy(f32[128,4,768]{2,0,1:T(8,128)S(1)} %fusion.27) | data formatting | bytes 3145728
  (7 shorter events, 0.2 us)
Async XLA Ops:
  3.7 11.4 %collective-permute-start = (f32[128,2,768]{2,1,0:T(2,128)S(1)}, f32[128,2,768]{2,1,0:T(2,128)S(1)}, u32[]{:S(2)}, u32[]{:S(2)}) collective-permute-start(f32[128,2,768]{2,1,0:T(2,128)S(1)} %get-tuple-element.18), channel_id=1, source_target_pairs={{1,0},{2,1},{3,2},{4,3},{5,4},{6,5},{7,6},{8,7},{9,8},{10,9},{11,1... | collective-permute-start | bytes 2359304 | tf_op jit(solution)/shard_map/ppermute | solution.py:26
  5.6 17.6 %collective-permute-start.1 = (f32[128,2,768]{2,1,0:T(2,128)S(1)}, f32[128,2,768]{2,1,0:T(2,128)S(1)}, u32[]{:S(2)}, u32[]{:S(2)}) collective-permute-start(f32[128,2,768]{2,1,0:T(2,128)S(1)} %get-tuple-element.19), channel_id=1, source_target_pairs={{0,1},{1,2},{2,3},{3,4},{4,5},{5,6},{6,7},{7,8},{8,9},{9,10},{10,1... | collective-permute-start | bytes 2359304 | tf_op jit(solution)/shard_map/ppermute | solution.py:25
  75.8 11.7 %collective-permute-start.2 = (f32[128,128]{1,0:T(8,128)S(1)}, f32[128,128]{1,0:T(8,128)S(1)}, u32[]{:S(2)}, u32[]{:S(2)}) collective-permute-start(f32[128,128]{1,0:T(8,128)S(1)} %fusion.20), channel_id=1, source_target_pairs={{0,128},{128,0},{256,384},{384,256},{1,129},{129,1},{257,385},{385... | collective-permute-start | bytes 196616 | tf_op jit(solution)/shard_map/ppermute | solution.py:89
  87.5 16.7 %collective-permute-start.3 = (f32[128,128]{1,0:T(8,128)S(1)}, f32[128,128]{1,0:T(8,128)S(1)}, u32[]{:S(2)}, u32[]{:S(2)}) collective-permute-start(f32[128,128]{1,0:T(8,128)S(1)} %fusion.35), channel_id=1, source_target_pairs={{0,256},{128,384},{256,0},{384,128},{1,257},{129,385},{257,1},{385... | collective-permute-start | bytes 196616 | tf_op jit(solution)/shard_map/ppermute | solution.py:89

commit v4 on v3

--- a/solution.py
+++ b/solution.py
@@ -41,18 +41,18 @@
         row = rest_ref[pl.ds(j, 1), :]
         ops_row = ops_ref[pl.ds(j, 1), :]
         pivot = jnp.sum(jnp.where(lane == j, row, 0.0), axis=1, keepdims=True)
-        root = jnp.sqrt(pivot)
-        factor_row = jnp.where(lane >= j, row / root, 0.0)
-        inverse_row = ops_row / root
+        scale = lax.rsqrt(pivot)
+        factor_row = jnp.where(lane >= j, row * scale, 0.0)
+        inverse_row = ops_row * scale
         upper_ref[pl.ds(j, 1), :] = factor_row
         inverse_ref[pl.ds(j, 1), :] = inverse_row
         column = jnp.sum(jnp.where(cols == j, rest, 0.0), axis=1, keepdims=True)
-        factor_col = jnp.where(sublane > j, column / root, 0.0)
+        factor_col = jnp.where(sublane > j, column * scale, 0.0)
         rest_ref[...] = rest - factor_col * factor_row
         ops_ref[...] = ops_ref[...] - factor_col * inverse_row
         return carry
 
-    lax.fori_loop(0, size, step, 0)
+    lax.fori_loop(0, size, step, 0, unroll=2)
 
 
 def factor(gram):
@@ -115,8 +115,9 @@
         comp_u = velocity[0]
         comp_v = velocity[1]
         padded = extended(comp_v, AXES, total, 1, 2)
+        u_second = lax.optimization_barrier(along_second(comp_u))
         v_first = stencil_rows(padded, row_count) / 12.0
-        vorticity = v_first - along_second(comp_u)
+        vorticity = v_first - u_second
         flattened = vorticity.reshape(snap_count, row_count * col_count)
         local_gram = (
             jnp.dot(

time: 125 us -> 123 us (0.984)
  waiting for transfers between devices: 32.1 us -> 29.2 us
    ppermute x1, waiting for transfers between devices: 4.85 us -> 2.07 us  [extended(): after = lax.ppermute(initial, axes, down)]
    div x0 -> x1, other arithmetic: none -> 2.77 us  [along_second(): (8.0 * (jnp.roll(field, -1, 2) - jnp.roll(field, 1, 2)) - (jnp.roll(field...]
    sub x1, other arithmetic: 4.88 us -> 2.87 us  [local(): vorticity = v_first - u_second]
  transfers between devices with their start and end apart: 4 -> 4, of which waited for: 4 -> 4; matrix products, arithmetic and copies ran while one was open for 2% -> 5% of each run, Pallas kernels for 0% -> 0%
where the time goes in v4:
time: 123 us; the launch traced here: 122 us
  blocking collectives  46.3 us (38%)
  waiting for transfers between devices  29.2 us (24%)
  Pallas kernels  14.9 us (12%)
  starting transfers between devices  12.5 us (10%)
  local copies, waits for them, and re-layouts  8.21 us (7%)
  other arithmetic  6.36 us (5%)
  matrix products  4.01 us (3%)
    all_to_all x3, blocking collectives, gather_sum(): gathered = lax.all_to_all(stacked, axes, 0, 0, tiled=True)  46.3 us
    ppermute x2, waiting for transfers between devices, butterfly_sum(): value = value + lax.ppermute(value, axis, pairs)  19 us
    pallas_call x1, Pallas kernels, factor(): pl.pallas_call(factor_kernel, out_shape=(jax.ShapeDtypeStruct((size, size...  14.9 us
    ppermute x2, starting transfers between devices, butterfly_sum(): value = value + lax.ppermute(value, axis, pairs)  8.22 us
    ppermute x1, waiting for transfers between devices, extended(): before = lax.ppermute(last, axes, up)  8.1 us
    sub x1, other arithmetic, local(): vorticity = v_first - u_second  2.87 us
    div x1, other arithmetic, along_second(): (8.0 * (jnp.roll(field, -1, 2) - jnp.roll(field, 1, 2)) - (jnp.roll(field...  2.77 us
  transfers between devices with their start and end apart: 4, of which 4 were waited for; matrix products, arithmetic and copies ran while one was open for 5% of the time, Pallas kernels for 0%

profile of v4, /device:TPU:2, one launch (start us, length us, event | category | flops | bytes accessed | tf_op | source)
XLA Modules:
  0.0 122.3 jit_solution(9453247331059541910)
XLA Ops:
  0.6 2.4 %slice_bitcast_fusion.1 = (f32[128,4,768]{2,1,0:T(4,128)S(1)}, f32[128,4,768]{2,1,0:T(4,128)S(1)}) fusion(f32[2,128,4,768]{3,2,1,0:T(4,128)} %param.1), kind=kLoop, calls=%fused_computation.22 | loop fusion | bytes 6291456 | tf_op jit(solution)/shard_map/squeeze | solution.py:116
  3.1 0.6 fusion.29
  3.7 1.9 %collective-permute-start = (f32[128,2,768]{2,1,0:T(2,128)S(1)}, f32[128,2,768]{2,1,0:T(2,128)S(1)}, u32[]{:S(2)}, u32[]{:S(2)}) collective-permute-start(f32[128,2,768]{2,1,0:T(2,128)S(1)} %get-tuple-element.10), channel_id=1, source_target_pairs={{1,0},{2,1},{3,2},{4,3},{5,4},{6,5},{7,6},{8,7},{9,8},{10,9},{11,1... | collective-permute-start | bytes 2359304 | tf_op jit(solution)/shard_map/ppermute | solution.py:26
  5.6 2.4 %collective-permute-start.1 = (f32[128,2,768]{2,1,0:T(2,128)S(1)}, f32[128,2,768]{2,1,0:T(2,128)S(1)}, u32[]{:S(2)}, u32[]{:S(2)}) collective-permute-start(f32[128,2,768]{2,1,0:T(2,128)S(1)} %get-tuple-element.11), channel_id=1, source_target_pairs={{0,1},{1,2},{2,3},{3,4},{4,5},{5,6},{6,7},{7,8},{8,9},{9,10},{10,1... | collective-permute-start | bytes 2359304 | tf_op jit(solution)/shard_map/ppermute | solution.py:25
  8.0 0.9 fusion.31
  8.9 0.2 fusion.30
  9.1 0.2 fusion.32
  9.3 0.9 fusion.33
  10.2 2.8 %fusion.10 = f32[128,4,768]{2,1,0:T(4,128)S(1)} fusion(f32[128,4,1]{2,1,0:T(4,128)S(1)} %get-tuple-element.17, f32[128,4,767]{2,1,0:T(4,128)S(1)} %get-tuple-element.19, f32[128,4,767]{2,1,0:T(4,128)S(1)} %get-tuple-element.18, f32[128,4,1]{2,1,0:T(4,128)S(1)} %get-tuple-element.16, f32[128,4,2]{2,1,0:T(4,128)S(1)} %get-tuple-element.13, ...), kind=kLoop, calls=%fused_computation.17 | loop fusion | flops 3538944 | bytes 7864320 | tf_op jit(solution)/shard_map/div | solution.py:95
  13.0 2.1 %collective-permute-done = f32[128,2,768]{2,1,0:T(2,128)S(1)} collective-permute-done((f32[128,2,768]{2,1,0:T(2,128)S(1)}, f32[128,2,768]{2,1,0:T(2,128)S(1)}, u32[]{:S(2)}, u32[]{:S(2)}) %collective-permute-start) | collective-permute-done | bytes 786464 | tf_op jit(solution)/shard_map/ppermute | solution.py:26
  15.1 8.1 %collective-permute-done.1 = f32[128,2,768]{2,1,0:T(2,128)S(1)} collective-permute-done((f32[128,2,768]{2,1,0:T(2,128)S(1)}, f32[128,2,768]{2,1,0:T(2,128)S(1)}, u32[]{:S(2)}, u32[]{:S(2)}) %collective-permute-start.1) | collective-permute-done | bytes 786464 | tf_op jit(solution)/shard_map/ppermute | solution.py:25
  23.2 2.9 %fusion.5 = f32[128,4,768]{2,1,0:T(4,128)S(1)} fusion(f32[128,4,768]{2,1,0:T(4,128)S(1)} %fusion.10, f32[128,2,768]{2,1,0:T(2,128)S(1)} %collective-permute-done.1, f32[128,4,768]{2,1,0:T(4,128)S(1)} %get-tuple-element.8, f32[128,2,768]{2,1,0:T(2,128)S(1)} %collective-permute-done), kind=kLoop, calls=%fused_computation.9 | loop fusion | flops 3932160 | bytes 6291456 | tf_op jit(solution)/shard_map/sub | solution.py:120
  26.1 1.7 %fusion.16 = f32[128,128]{1,0:T(8,128)S(1)} fusion(f32[128,4,768]{2,1,0:T(4,128)S(1)} %fusion.5), kind=kOutput, calls=%fused_computation.24 | convolution fusion | flops 603996160 | bytes 1638400 | tf_op jit(solution)/shard_map/dot_general | solution.py:123
  27.8 27.0 %all_to_all.15 = f32[8,128,128]{2,1,0:T(8,128)S(1)} all-to-all(f32[8,128,128]{2,1,0:T(8,128)S(1)} %broadcast_in_dim.10), channel_id=1, replica_groups=mesh['zh'=4,'zl'=4,'y'=4,'x'=4,'core'=2] {'x','core'}, dimensions={0} | all-to-all | bytes 1048576 | tf_op jit(solution)/shard_map/all_to_all | solution.py:81
  54.9 9.1 %all_to_all.16 = f32[4,128,128]{2,1,0:T(8,128)S(1)} all-to-all(f32[4,128,128]{2,1,0:T(8,128)S(1)} %broadcast_in_dim.24), channel_id=1, replica_groups=mesh['zh'=4,'zl'=4,'y'=4,'x'=4,'core'=2] {'y'}, dimensions={0} | all-to-all | bytes 524288 | tf_op jit(solution)/shard_map/all_to_all | solution.py:81
  64.0 10.2 %all_to_all.17 = f32[4,128,128]{2,1,0:T(8,128)S(1)} all-to-all(f32[4,128,128]{2,1,0:T(8,128)S(1)} %broadcast_in_dim.26), channel_id=1, replica_groups=mesh['zh'=4,'zl'=4,'y'=4,'x'=4,'core'=2] {'zl'}, dimensions={0} | all-to-all | bytes 524288 | tf_op jit(solution)/shard_map/all_to_all | solution.py:81
  74.2 1.9 %collective-permute-start.2 = (f32[128,128]{1,0:T(8,128)S(1)}, f32[128,128]{1,0:T(8,128)S(1)}, u32[]{:S(2)}, u32[]{:S(2)}) collective-permute-start(f32[128,128]{1,0:T(8,128)S(1)} %fusion.20), channel_id=1, source_target_pairs={{0,128},{128,0},{256,384},{384,256},{1,129},{129,1},{257,385},{385... | collective-permute-start | bytes 196616 | tf_op jit(solution)/shard_map/ppermute | solution.py:89
  76.2 9.7 %collective-permute-done.2 = f32[128,128]{1,0:T(8,128)S(1)} collective-permute-done((f32[128,128]{1,0:T(8,128)S(1)}, f32[128,128]{1,0:T(8,128)S(1)}, u32[]{:S(2)}, u32[]{:S(2)}) %collective-permute-start.2) | collective-permute-done | bytes 65568 | tf_op jit(solution)/shard_map/ppermute | solution.py:89
  85.9 6.3 %collective-permute-start.3 = (f32[128,128]{1,0:T(8,128)S(1)}, f32[128,128]{1,0:T(8,128)S(1)}, u32[]{:S(2)}, u32[]{:S(2)}) collective-permute-start(f32[128,128]{1,0:T(8,128)S(1)} %fusion.35), channel_id=1, source_target_pairs={{0,256},{128,384},{256,0},{384,128},{1,257},{129,385},{257,1},{385... | collective-permute-start | bytes 196616 | tf_op jit(solution)/shard_map/ppermute | solution.py:89
  92.2 0.3 copy.7
  92.5 0.5 copy.5
  93.0 9.3 %collective-permute-done.3 = f32[128,128]{1,0:T(8,128)S(1)} collective-permute-done((f32[128,128]{1,0:T(8,128)S(1)}, f32[128,128]{1,0:T(8,128)S(1)}, u32[]{:S(2)}, u32[]{:S(2)}) %collective-permute-start.3) | collective-permute-done | bytes 65568 | tf_op jit(solution)/shard_map/ppermute | solution.py:89
  102.2 0.6 add.75.gram_ref
  102.9 14.9 %shard_map.30 = (f32[128,128]{1,0:T(8,128)}, f32[128,128]{1,0:T(8,128)}) custom-call(f32[128,128]{1,0:T(8,128)} %add.75.gram_ref), custom_call_target="tpu_custom_call" | custom-call | tf_op jit(solution)/shard_map/pallas_call | solution.py:61
  117.8 2.3 %fusion.27 = f32[128,4,768]{2,0,1:T(8,128)S(1)} fusion(f32[4,768,128]{2,1,0:T(8,128)S(1)} %bitcast.26, f32[128,128]{1,0:T(8,128)} %get-tuple-element.4), kind=kOutput, calls=%fused_computation.41 | convolution fusion | flops 603979776 | bytes 3211264 | tf_op jit(solution)/shard_map/dot_general | solution.py:136
  120.1 2.2 %copy.6 = f32[128,4,768]{2,1,0:T(4,128)} copy(f32[128,4,768]{2,0,1:T(8,128)S(1)} %fusion.27) | data formatting | bytes 3145728
  (7 shorter events, 0.2 us)
Async XLA Ops:
  3.7 11.4 %collective-permute-start = (f32[128,2,768]{2,1,0:T(2,128)S(1)}, f32[128,2,768]{2,1,0:T(2,128)S(1)}, u32[]{:S(2)}, u32[]{:S(2)}) collective-permute-start(f32[128,2,768]{2,1,0:T(2,128)S(1)} %get-tuple-element.10), channel_id=1, source_target_pairs={{1,0},{2,1},{3,2},{4,3},{5,4},{6,5},{7,6},{8,7},{9,8},{10,9},{11,1... | collective-permute-start | bytes 2359304 | tf_op jit(solution)/shard_map/ppermute | solution.py:26
  5.6 17.6 %collective-permute-start.1 = (f32[128,2,768]{2,1,0:T(2,128)S(1)}, f32[128,2,768]{2,1,0:T(2,128)S(1)}, u32[]{:S(2)}, u32[]{:S(2)}) collective-permute-start(f32[128,2,768]{2,1,0:T(2,128)S(1)} %get-tuple-element.11), channel_id=1, source_target_pairs={{0,1},{1,2},{2,3},{3,4},{4,5},{5,6},{6,7},{7,8},{8,9},{9,10},{10,1... | collective-permute-start | bytes 2359304 | tf_op jit(solution)/shard_map/ppermute | solution.py:25
  74.2 11.7 %collective-permute-start.2 = (f32[128,128]{1,0:T(8,128)S(1)}, f32[128,128]{1,0:T(8,128)S(1)}, u32[]{:S(2)}, u32[]{:S(2)}) collective-permute-start(f32[128,128]{1,0:T(8,128)S(1)} %fusion.20), channel_id=1, source_target_pairs={{0,128},{128,0},{256,384},{384,256},{1,129},{129,1},{257,385},{385... | collective-permute-start | bytes 196616 | tf_op jit(solution)/shard_map/ppermute | solution.py:89
  85.9 16.3 %collective-permute-start.3 = (f32[128,128]{1,0:T(8,128)S(1)}, f32[128,128]{1,0:T(8,128)S(1)}, u32[]{:S(2)}, u32[]{:S(2)}) collective-permute-start(f32[128,128]{1,0:T(8,128)S(1)} %fusion.35), channel_id=1, source_target_pairs={{0,256},{128,384},{256,0},{384,128},{1,257},{129,385},{257,1},{385... | collective-permute-start | bytes 196616 | tf_op jit(solution)/shard_map/ppermute | solution.py:89

commit v5 on v4

--- a/solution.py
+++ b/solution.py
@@ -70,6 +70,31 @@
     )(gram)
 
 
+def pack_symmetric(gram):
+    half = gram.shape[0] // 2
+    rows = lax.broadcasted_iota(jnp.int32, (half, half), 0)
+    cols = lax.broadcasted_iota(jnp.int32, (half, half), 1)
+    top, corner, bottom = gram[:half, :half], gram[:half, half:], gram[half:, half:]
+    folded = jnp.where(rows <= cols, top, bottom)
+    diagonal = jnp.sum(jnp.where(rows == cols, bottom, 0.0), axis=0, keepdims=True)
+    tail = jnp.concatenate([diagonal, jnp.zeros_like(diagonal)], axis=1)
+    return jnp.concatenate([jnp.concatenate([corner, folded], axis=1), tail], axis=0)
+
+
+def unpack_symmetric(packed):
+    half = packed.shape[1] // 2
+    rows = lax.broadcasted_iota(jnp.int32, (half, half), 0)
+    cols = lax.broadcasted_iota(jnp.int32, (half, half), 1)
+    corner, folded = packed[:half, :half], packed[:half, half:]
+    diagonal = packed[half : half + 1, :half]
+    flipped = folded.T
+    top = jnp.where(rows <= cols, folded, flipped)
+    bottom = jnp.where(rows > cols, folded, jnp.where(rows < cols, flipped, diagonal))
+    upper = jnp.concatenate([top, corner], axis=1)
+    lower = jnp.concatenate([corner.T, bottom], axis=1)
+    return jnp.concatenate([upper, lower], axis=0)
+
+
 def tree_sum(values):
     while len(values) > 1:
         values = [values[i] + values[i + 1] for i in range(0, len(values), 2)]
@@ -128,10 +153,12 @@
             )
             / total_cells
         )
-        gram = gather_sum(local_gram, ("x", "core"), sizes["x"] * sizes["core"])
+        gram = pack_symmetric(local_gram)
+        gram = gather_sum(gram, ("x", "core"), sizes["x"] * sizes["core"])
         gram = gather_sum(gram, ("y",), sizes["y"])
         gram = gather_sum(gram, ("zl",), sizes["zl"])
         gram = butterfly_sum(gram, "zh", sizes["zh"])
+        gram = unpack_symmetric(gram)
         upper, inverse_lower = factor(gram)
         spatial_modes = jnp.dot(
             inverse_lower,

time: 123 us -> 116 us (0.943)
  blocking collectives: 46.3 us -> 41.8 us
  waiting for transfers between devices: 29.2 us -> 26.6 us
    all_to_all x3, blocking collectives: 46.3 us -> 41.8 us  [gather_sum(): gathered = lax.all_to_all(stacked, axes, 0, 0, tiled=True)]
    ppermute x2, waiting for transfers between devices: 19 us -> 16.4 us  [butterfly_sum(): value = value + lax.ppermute(value, axis, pairs)]
where the time goes in v5:
time: 116 us
  blocking collectives  41.8 us (36%)
  waiting for transfers between devices  26.6 us (23%)
  Pallas kernels  14.9 us (13%)
  starting transfers between devices  12.8 us (11%)
  local copies, waits for them, and re-layouts  8.41 us (7%)
  other arithmetic  6.69 us (6%)
  matrix products  4.01 us (3%)
    all_to_all x3, blocking collectives, gather_sum(): gathered = lax.all_to_all(stacked, axes, 0, 0, tiled=True)  41.8 us
    ppermute x2, waiting for transfers between devices, butterfly_sum(): value = value + lax.ppermute(value, axis, pairs)  16.4 us
    pallas_call x1, Pallas kernels, factor(): pl.pallas_call(factor_kernel, out_shape=(jax.ShapeDtypeStruct((size, size...  14.9 us
    ppermute x2, starting transfers between devices, butterfly_sum(): value = value + lax.ppermute(value, axis, pairs)  8.51 us
    ppermute x1, waiting for transfers between devices, extended(): before = lax.ppermute(last, axes, up)  8.1 us
    sub x1, other arithmetic, local(): vorticity = v_first - u_second  2.87 us
    div x1, other arithmetic, along_second(): (8.0 * (jnp.roll(field, -1, 2) - jnp.roll(field, 1, 2)) - (jnp.roll(field...  2.77 us
    unnamed x2, local copies, waits for them, and re-layouts  2.43 us
  transfers between devices with their start and end apart: 4, of which 4 were waited for; matrix products, arithmetic and copies ran while one was open for 5% of the time, Pallas kernels for 0%

profile of v5, /device:TPU:2, one launch (start us, length us, event | category | flops | bytes accessed | tf_op | source)
XLA Modules:
  0.0 116.0 jit_solution(1831274335346207240)
XLA Ops:
  0.6 2.4 %slice_bitcast_fusion.1 = (f32[128,4,768]{2,1,0:T(4,128)S(1)}, f32[128,4,768]{2,1,0:T(4,128)S(1)}) fusion(f32[2,128,4,768]{3,2,1,0:T(4,128)} %param.1), kind=kLoop, calls=%fused_computation.22 | loop fusion | bytes 6291456 | tf_op jit(solution)/shard_map/squeeze | solution.py:141
  3.1 0.6 fusion.30
  3.7 1.9 %collective-permute-start = (f32[128,2,768]{2,1,0:T(2,128)S(1)}, f32[128,2,768]{2,1,0:T(2,128)S(1)}, u32[]{:S(2)}, u32[]{:S(2)}) collective-permute-start(f32[128,2,768]{2,1,0:T(2,128)S(1)} %get-tuple-element.10), channel_id=1, source_target_pairs={{1,0},{2,1},{3,2},{4,3},{5,4},{6,5},{7,6},{8,7},{9,8},{10,9},{11,1... | collective-permute-start | bytes 2359304 | tf_op jit(solution)/shard_map/ppermute | solution.py:26
  5.6 2.4 %collective-permute-start.1 = (f32[128,2,768]{2,1,0:T(2,128)S(1)}, f32[128,2,768]{2,1,0:T(2,128)S(1)}, u32[]{:S(2)}, u32[]{:S(2)}) collective-permute-start(f32[128,2,768]{2,1,0:T(2,128)S(1)} %get-tuple-element.11), channel_id=1, source_target_pairs={{0,1},{1,2},{2,3},{3,4},{4,5},{5,6},{6,7},{7,8},{8,9},{9,10},{10,1... | collective-permute-start | bytes 2359304 | tf_op jit(solution)/shard_map/ppermute | solution.py:25
  8.0 0.9 fusion.32
  8.9 0.2 fusion.31
  9.1 0.2 fusion.33
  9.3 0.9 fusion.34
  10.2 2.8 %fusion.10 = f32[128,4,768]{2,1,0:T(4,128)S(1)} fusion(f32[128,4,1]{2,1,0:T(4,128)S(1)} %get-tuple-element.17, f32[128,4,767]{2,1,0:T(4,128)S(1)} %get-tuple-element.19, f32[128,4,767]{2,1,0:T(4,128)S(1)} %get-tuple-element.18, f32[128,4,1]{2,1,0:T(4,128)S(1)} %get-tuple-element.16, f32[128,4,2]{2,1,0:T(4,128)S(1)} %get-tuple-element.13, ...), kind=kLoop, calls=%fused_computation.17 | loop fusion | flops 3538944 | bytes 7864320 | tf_op jit(solution)/shard_map/div | solution.py:120
  13.0 2.1 %collective-permute-done = f32[128,2,768]{2,1,0:T(2,128)S(1)} collective-permute-done((f32[128,2,768]{2,1,0:T(2,128)S(1)}, f32[128,2,768]{2,1,0:T(2,128)S(1)}, u32[]{:S(2)}, u32[]{:S(2)}) %collective-permute-start) | collective-permute-done | bytes 786464 | tf_op jit(solution)/shard_map/ppermute | solution.py:26
  15.1 8.1 %collective-permute-done.1 = f32[128,2,768]{2,1,0:T(2,128)S(1)} collective-permute-done((f32[128,2,768]{2,1,0:T(2,128)S(1)}, f32[128,2,768]{2,1,0:T(2,128)S(1)}, u32[]{:S(2)}, u32[]{:S(2)}) %collective-permute-start.1) | collective-permute-done | bytes 786464 | tf_op jit(solution)/shard_map/ppermute | solution.py:25
  23.2 2.9 %fusion.5 = f32[128,4,768]{2,1,0:T(4,128)S(1)} fusion(f32[128,4,768]{2,1,0:T(4,128)S(1)} %fusion.10, f32[128,2,768]{2,1,0:T(2,128)S(1)} %collective-permute-done.1, f32[128,4,768]{2,1,0:T(4,128)S(1)} %get-tuple-element.8, f32[128,2,768]{2,1,0:T(2,128)S(1)} %collective-permute-done), kind=kLoop, calls=%fused_computation.9 | loop fusion | flops 3932160 | bytes 6291456 | tf_op jit(solution)/shard_map/sub | solution.py:145
  26.1 1.7 %fusion.16 = f32[128,128]{1,0:T(8,128)S(1)} fusion(f32[128,4,768]{2,1,0:T(4,128)S(1)} %fusion.5), kind=kOutput, calls=%fused_computation.24 | convolution fusion | flops 603996160 | bytes 1638400 | tf_op jit(solution)/shard_map/dot_general | solution.py:148
  27.8 0.1 fusion.35
  27.9 0.1 select_maximum_fusion
  28.0 24.3 %all_to_all.15 = f32[8,65,128]{2,1,0:T(8,128)S(1)} all-to-all(f32[8,65,128]{2,1,0:T(8,128)S(1)} %broadcast_in_dim.42), channel_id=1, replica_groups=mesh['zh'=4,'zl'=4,'y'=4,'x'=4,'core'=2] {'x','core'}, dimensions={0} | all-to-all | bytes 532480 | tf_op jit(solution)/shard_map/all_to_all | solution.py:106
  52.3 8.4 %all_to_all.16 = f32[4,65,128]{2,1,0:T(8,128)S(1)} all-to-all(f32[4,65,128]{2,1,0:T(8,128)S(1)} %broadcast_in_dim.44), channel_id=1, replica_groups=mesh['zh'=4,'zl'=4,'y'=4,'x'=4,'core'=2] {'y'}, dimensions={0} | all-to-all | bytes 266240 | tf_op jit(solution)/shard_map/all_to_all | solution.py:106
  60.8 9.0 %all_to_all.17 = f32[4,65,128]{2,1,0:T(8,128)S(1)} all-to-all(f32[4,65,128]{2,1,0:T(8,128)S(1)} %broadcast_in_dim.46), channel_id=1, replica_groups=mesh['zh'=4,'zl'=4,'y'=4,'x'=4,'core'=2] {'zl'}, dimensions={0} | all-to-all | bytes 266240 | tf_op jit(solution)/shard_map/all_to_all | solution.py:106
  69.8 1.9 %collective-permute-start.2 = (f32[65,128]{1,0:T(8,128)S(1)}, f32[65,128]{1,0:T(8,128)S(1)}, u32[]{:S(2)}, u32[]{:S(2)}) collective-permute-start(f32[65,128]{1,0:T(8,128)S(1)} %fusion.22), channel_id=1, source_target_pairs={{0,128},{128,0},{256,384},{384,256},{1,129},{129,1},{257,385},{385... | collective-permute-start | bytes 99848 | tf_op jit(solution)/shard_map/ppermute | solution.py:114
  71.7 9.0 %collective-permute-done.2 = f32[65,128]{1,0:T(8,128)S(1)} collective-permute-done((f32[65,128]{1,0:T(8,128)S(1)}, f32[65,128]{1,0:T(8,128)S(1)}, u32[]{:S(2)}, u32[]{:S(2)}) %collective-permute-start.2) | collective-permute-done | bytes 33312 | tf_op jit(solution)/shard_map/ppermute | solution.py:114
  80.8 6.6 %collective-permute-start.3 = (f32[65,128]{1,0:T(8,128)S(1)}, f32[65,128]{1,0:T(8,128)S(1)}, u32[]{:S(2)}, u32[]{:S(2)}) collective-permute-start(f32[65,128]{1,0:T(8,128)S(1)} %fusion.37), channel_id=1, source_target_pairs={{0,256},{128,384},{256,0},{384,128},{1,257},{129,385},{257,1},{385... | collective-permute-start | bytes 99848 | tf_op jit(solution)/shard_map/ppermute | solution.py:114
  87.4 0.3 copy.9
  87.7 0.5 copy.7
  88.1 7.4 %collective-permute-done.3 = f32[65,128]{1,0:T(8,128)S(1)} collective-permute-done((f32[65,128]{1,0:T(8,128)S(1)}, f32[65,128]{1,0:T(8,128)S(1)}, u32[]{:S(2)}, u32[]{:S(2)}) %collective-permute-start.3) | collective-permute-done | bytes 33312 | tf_op jit(solution)/shard_map/ppermute | solution.py:114
  95.5 0.1 slice.197
  95.6 0.1 copy.5
  95.7 0.1 bitcast_select_fusion.1
  95.8 0.1 copy.6
  95.8 0.7 maximum_maximum_fusion.gram_ref
  96.6 14.9 %shard_map.30 = (f32[128,128]{1,0:T(8,128)}, f32[128,128]{1,0:T(8,128)}) custom-call(f32[128,128]{1,0:T(8,128)} %maximum_maximum_fusion.gram_ref), custom_call_target="tpu_custom_call" | custom-call | tf_op jit(solution)/shard_map/pallas_call | solution.py:61
  111.5 2.3 %fusion.19 = f32[128,4,768]{2,0,1:T(8,128)S(1)} fusion(f32[4,768,128]{2,1,0:T(8,128)S(1)} %bitcast.36, f32[128,128]{1,0:T(8,128)} %get-tuple-element.4), kind=kOutput, calls=%fused_computation.26 | convolution fusion | flops 603979776 | bytes 3211264 | tf_op jit(solution)/shard_map/dot_general | solution.py:163
  113.8 2.2 %copy.8 = f32[128,4,768]{2,1,0:T(4,128)} copy(f32[128,4,768]{2,0,1:T(8,128)S(1)} %fusion.19) | data formatting | bytes 3145728
  (9 shorter events, 0.1 us)
Async XLA Ops:
  3.7 11.4 %collective-permute-start = (f32[128,2,768]{2,1,0:T(2,128)S(1)}, f32[128,2,768]{2,1,0:T(2,128)S(1)}, u32[]{:S(2)}, u32[]{:S(2)}) collective-permute-start(f32[128,2,768]{2,1,0:T(2,128)S(1)} %get-tuple-element.10), channel_id=1, source_target_pairs={{1,0},{2,1},{3,2},{4,3},{5,4},{6,5},{7,6},{8,7},{9,8},{10,9},{11,1... | collective-permute-start | bytes 2359304 | tf_op jit(solution)/shard_map/ppermute | solution.py:26
  5.6 17.6 %collective-permute-start.1 = (f32[128,2,768]{2,1,0:T(2,128)S(1)}, f32[128,2,768]{2,1,0:T(2,128)S(1)}, u32[]{:S(2)}, u32[]{:S(2)}) collective-permute-start(f32[128,2,768]{2,1,0:T(2,128)S(1)} %get-tuple-element.11), channel_id=1, source_target_pairs={{0,1},{1,2},{2,3},{3,4},{4,5},{5,6},{6,7},{7,8},{8,9},{9,10},{10,1... | collective-permute-start | bytes 2359304 | tf_op jit(solution)/shard_map/ppermute | solution.py:25
  69.8 10.9 %collective-permute-start.2 = (f32[65,128]{1,0:T(8,128)S(1)}, f32[65,128]{1,0:T(8,128)S(1)}, u32[]{:S(2)}, u32[]{:S(2)}) collective-permute-start(f32[65,128]{1,0:T(8,128)S(1)} %fusion.22), channel_id=1, source_target_pairs={{0,128},{128,0},{256,384},{384,256},{1,129},{129,1},{257,385},{385... | collective-permute-start | bytes 99848 | tf_op jit(solution)/shard_map/ppermute | solution.py:114
  80.8 14.7 %collective-permute-start.3 = (f32[65,128]{1,0:T(8,128)S(1)}, f32[65,128]{1,0:T(8,128)S(1)}, u32[]{:S(2)}, u32[]{:S(2)}) collective-permute-start(f32[65,128]{1,0:T(8,128)S(1)} %fusion.37), channel_id=1, source_target_pairs={{0,256},{128,384},{256,0},{384,128},{1,257},{129,385},{257,1},{385... | collective-permute-start | bytes 99848 | tf_op jit(solution)/shard_map/ppermute | solution.py:114

commit v6 on v5

--- a/solution.py
+++ b/solution.py
@@ -157,7 +157,7 @@
         gram = gather_sum(gram, ("x", "core"), sizes["x"] * sizes["core"])
         gram = gather_sum(gram, ("y",), sizes["y"])
         gram = gather_sum(gram, ("zl",), sizes["zl"])
-        gram = butterfly_sum(gram, "zh", sizes["zh"])
+        gram = gather_sum(gram, ("zh",), sizes["zh"])
         gram = unpack_symmetric(gram)
         upper, inverse_lower = factor(gram)
         spatial_modes = jnp.dot(

time: 116 us -> 111 us (0.957)
  the two profiles are of different devices: /device:TPU:2 before, /device:TPU:32 now
where the time goes in v6:
time: 111 us
  blocking collectives  37.3 us (34%)
  waiting for transfers between devices  24.1 us (22%)
  Pallas kernels  14.9 us (13%)
  starting transfers between devices  13.8 us (12%)
  local copies, waits for them, and re-layouts  9.08 us (8%)
  other arithmetic  6.68 us (6%)
  matrix products  4.01 us (4%)
    all_to_all x3, blocking collectives, gather_sum(): gathered = lax.all_to_all(stacked, axes, 0, 0, tiled=True)  37.3 us
    pallas_call x1, Pallas kernels, factor(): pl.pallas_call(factor_kernel, out_shape=(jax.ShapeDtypeStruct((size, size...  14.9 us
    all_to_all x1, waiting for transfers between devices, gather_sum(): gathered = lax.all_to_all(stacked, axes, 0, 0, tiled=True)  13.5 us
    ppermute x1, waiting for transfers between devices, extended(): before = lax.ppermute(last, axes, up)  8.04 us
    ppermute x1, starting transfers between devices, extended(): after = lax.ppermute(initial, axes, down)  6.1 us
    all_to_all x1, starting transfers between devices, gather_sum(): gathered = lax.all_to_all(stacked, axes, 0, 0, tiled=True)  5.77 us
    sub x1, other arithmetic, local(): vorticity = v_first - u_second  2.87 us
    div x1, other arithmetic, along_second(): (8.0 * (jnp.roll(field, -1, 2) - jnp.roll(field, 1, 2)) - (jnp.roll(field...  2.77 us
  transfers between devices with their start and end apart: 3, of which 3 were waited for; matrix products, arithmetic and copies ran while one was open for 5% of the time, Pallas kernels for 0%

profile of v6, /device:TPU:32, one launch (start us, length us, event | category | flops | bytes accessed | tf_op | source)
XLA Modules:
  0.0 110.6 jit_solution(7245633147666151756)
XLA Ops:
  0.6 2.4 %slice_bitcast_fusion.1 = (f32[128,4,768]{2,1,0:T(4,128)S(1)}, f32[128,4,768]{2,1,0:T(4,128)S(1)}) fusion(f32[2,128,4,768]{3,2,1,0:T(4,128)} %param.1), kind=kLoop, calls=%fused_computation.22 | loop fusion | bytes 6291456 | tf_op jit(solution)/shard_map/squeeze | solution.py:141
  3.1 0.6 fusion.32
  3.7 6.1 %collective-permute-start = (f32[128,2,768]{2,1,0:T(2,128)S(1)}, f32[128,2,768]{2,1,0:T(2,128)S(1)}, u32[]{:S(2)}, u32[]{:S(2)}) collective-permute-start(f32[128,2,768]{2,1,0:T(2,128)S(1)} %get-tuple-element.10), channel_id=1, source_target_pairs={{1,0},{2,1},{3,2},{4,3},{5,4},{6,5},{7,6},{8,7},{9,8},{10,9},{11,1... | collective-permute-start | bytes 2359304 | tf_op jit(solution)/shard_map/ppermute | solution.py:26
  9.8 1.9 %collective-permute-start.1 = (f32[128,2,768]{2,1,0:T(2,128)S(1)}, f32[128,2,768]{2,1,0:T(2,128)S(1)}, u32[]{:S(2)}, u32[]{:S(2)}) collective-permute-start(f32[128,2,768]{2,1,0:T(2,128)S(1)} %get-tuple-element.11), channel_id=1, source_target_pairs={{0,1},{1,2},{2,3},{3,4},{4,5},{5,6},{6,7},{7,8},{8,9},{9,10},{10,1... | collective-permute-start | bytes 2359304 | tf_op jit(solution)/shard_map/ppermute | solution.py:25
  11.7 0.9 fusion.34
  12.6 0.2 fusion.33
  12.8 0.2 fusion.35
  13.0 0.9 fusion.36
  13.9 2.8 %fusion.10 = f32[128,4,768]{2,1,0:T(4,128)S(1)} fusion(f32[128,4,1]{2,1,0:T(4,128)S(1)} %get-tuple-element.17, f32[128,4,767]{2,1,0:T(4,128)S(1)} %get-tuple-element.19, f32[128,4,767]{2,1,0:T(4,128)S(1)} %get-tuple-element.18, f32[128,4,1]{2,1,0:T(4,128)S(1)} %get-tuple-element.16, f32[128,4,2]{2,1,0:T(4,128)S(1)} %get-tuple-element.13, ...), kind=kLoop, calls=%fused_computation.17 | loop fusion | flops 3538944 | bytes 7864320 | tf_op jit(solution)/shard_map/div | solution.py:120
  16.7 2.6 %collective-permute-done = f32[128,2,768]{2,1,0:T(2,128)S(1)} collective-permute-done((f32[128,2,768]{2,1,0:T(2,128)S(1)}, f32[128,2,768]{2,1,0:T(2,128)S(1)}, u32[]{:S(2)}, u32[]{:S(2)}) %collective-permute-start) | collective-permute-done | bytes 786464 | tf_op jit(solution)/shard_map/ppermute | solution.py:26
  19.3 8.0 %collective-permute-done.1 = f32[128,2,768]{2,1,0:T(2,128)S(1)} collective-permute-done((f32[128,2,768]{2,1,0:T(2,128)S(1)}, f32[128,2,768]{2,1,0:T(2,128)S(1)}, u32[]{:S(2)}, u32[]{:S(2)}) %collective-permute-start.1) | collective-permute-done | bytes 786464 | tf_op jit(solution)/shard_map/ppermute | solution.py:25
  27.3 2.9 %fusion.5 = f32[128,4,768]{2,1,0:T(4,128)S(1)} fusion(f32[128,4,768]{2,1,0:T(4,128)S(1)} %fusion.10, f32[128,2,768]{2,1,0:T(2,128)S(1)} %collective-permute-done.1, f32[128,4,768]{2,1,0:T(4,128)S(1)} %get-tuple-element.8, f32[128,2,768]{2,1,0:T(2,128)S(1)} %collective-permute-done), kind=kLoop, calls=%fused_computation.9 | loop fusion | flops 3932160 | bytes 6291456 | tf_op jit(solution)/shard_map/sub | solution.py:145
  30.2 1.7 %fusion.16 = f32[128,128]{1,0:T(8,128)S(1)} fusion(f32[128,4,768]{2,1,0:T(4,128)S(1)} %fusion.5), kind=kOutput, calls=%fused_computation.24 | convolution fusion | flops 603996160 | bytes 1638400 | tf_op jit(solution)/shard_map/dot_general | solution.py:148
  31.9 0.1 fusion.37
  32.0 0.1 select_maximum_fusion
  32.1 10.3 %all_to_all.20 = f32[8,65,128]{2,1,0:T(8,128)S(1)} all-to-all(f32[8,65,128]{2,1,0:T(8,128)S(1)} %broadcast_in_dim.50), channel_id=1, replica_groups=mesh['zh'=4,'zl'=4,'y'=4,'x'=4,'core'=2] {'x','core'}, dimensions={0} | all-to-all | bytes 532480 | tf_op jit(solution)/shard_map/all_to_all | solution.py:106
  42.4 8.4 %all_to_all.21 = f32[4,65,128]{2,1,0:T(8,128)S(1)} all-to-all(f32[4,65,128]{2,1,0:T(8,128)S(1)} %broadcast_in_dim.52), channel_id=1, replica_groups=mesh['zh'=4,'zl'=4,'y'=4,'x'=4,'core'=2] {'y'}, dimensions={0} | all-to-all | bytes 266240 | tf_op jit(solution)/shard_map/all_to_all | solution.py:106
  50.8 18.6 %all_to_all.22 = f32[4,65,128]{2,1,0:T(8,128)S(1)} all-to-all(f32[4,65,128]{2,1,0:T(8,128)S(1)} %broadcast_in_dim.54), channel_id=1, replica_groups=mesh['zh'=4,'zl'=4,'y'=4,'x'=4,'core'=2] {'zl'}, dimensions={0} | all-to-all | bytes 266240 | tf_op jit(solution)/shard_map/all_to_all | solution.py:106
  69.5 0.7 broadcast_in_dim.56
  70.1 5.8 %all-to-all-start.3 = ((f32[4,65,128]{2,1,0:T(8,128)}), f32[4,65,128]{2,1,0:T(8,128)S(1)}, u32[]{:S(2)}, u32[]{:S(2)}) async-start(f32[4,65,128]{2,1,0:T(8,128)} %broadcast_in_dim.56), calls=%async_computation.3 | async-start | bytes 294912 | tf_op jit(solution)/shard_map/all_to_all | solution.py:106
  75.9 0.3 copy.9
  76.2 0.5 copy.7
  76.7 13.5 %all-to-all-done.3 = f32[4,65,128]{2,1,0:T(8,128)S(1)} async-done(((f32[4,65,128]{2,1,0:T(8,128)}), f32[4,65,128]{2,1,0:T(8,128)S(1)}, u32[]{:S(2)}, u32[]{:S(2)}) %all-to-all-start.3) | async-done | bytes 133152 | tf_op jit(solution)/shard_map/all_to_all | solution.py:106
  90.2 0.1 slice.217
  90.3 0.1 copy.5
  90.3 0.1 bitcast_select_fusion.1
  90.4 0.1 copy.6
  90.5 0.7 maximum_maximum_fusion.gram_ref
  91.2 14.9 %shard_map.30 = (f32[128,128]{1,0:T(8,128)}, f32[128,128]{1,0:T(8,128)}) custom-call(f32[128,128]{1,0:T(8,128)} %maximum_maximum_fusion.gram_ref), custom_call_target="tpu_custom_call" | custom-call | tf_op jit(solution)/shard_map/pallas_call | solution.py:61
  106.2 2.3 %fusion.19 = f32[128,4,768]{2,0,1:T(8,128)S(1)} fusion(f32[4,768,128]{2,1,0:T(8,128)S(1)} %bitcast.36, f32[128,128]{1,0:T(8,128)} %get-tuple-element.4), kind=kOutput, calls=%fused_computation.26 | convolution fusion | flops 603979776 | bytes 3211264 | tf_op jit(solution)/shard_map/dot_general | solution.py:163
  108.5 2.2 %copy.8 = f32[128,4,768]{2,1,0:T(4,128)} copy(f32[128,4,768]{2,0,1:T(8,128)S(1)} %fusion.19) | data formatting | bytes 3145728
  (8 shorter events, 0.1 us)
Async XLA Ops:
  3.7 15.6 %collective-permute-start = (f32[128,2,768]{2,1,0:T(2,128)S(1)}, f32[128,2,768]{2,1,0:T(2,128)S(1)}, u32[]{:S(2)}, u32[]{:S(2)}) collective-permute-start(f32[128,2,768]{2,1,0:T(2,128)S(1)} %get-tuple-element.10), channel_id=1, source_target_pairs={{1,0},{2,1},{3,2},{4,3},{5,4},{6,5},{7,6},{8,7},{9,8},{10,9},{11,1... | collective-permute-start | bytes 2359304 | tf_op jit(solution)/shard_map/ppermute | solution.py:26
  9.8 17.5 %collective-permute-start.1 = (f32[128,2,768]{2,1,0:T(2,128)S(1)}, f32[128,2,768]{2,1,0:T(2,128)S(1)}, u32[]{:S(2)}, u32[]{:S(2)}) collective-permute-start(f32[128,2,768]{2,1,0:T(2,128)S(1)} %get-tuple-element.11), channel_id=1, source_target_pairs={{0,1},{1,2},{2,3},{3,4},{4,5},{5,6},{6,7},{7,8},{8,9},{9,10},{10,1... | collective-permute-start | bytes 2359304 | tf_op jit(solution)/shard_map/ppermute | solution.py:25
  70.1 20.0 %all-to-all-start.3 = ((f32[4,65,128]{2,1,0:T(8,128)}), f32[4,65,128]{2,1,0:T(8,128)S(1)}, u32[]{:S(2)}, u32[]{:S(2)}) async-start(f32[4,65,128]{2,1,0:T(8,128)} %broadcast_in_dim.56), calls=%async_computation.3 | async-start | bytes 294912 | tf_op jit(solution)/shard_map/all_to_all | solution.py:106

commit v7 on v6

--- a/solution.py
+++ b/solution.py
@@ -16,15 +16,15 @@
     return size
 
 
-def extended(array, axes, size, dim, width):
-    length = array.shape[dim]
+def halo(velocity, axes, size, width):
+    length = velocity.shape[2]
     up = [(i, (i + 1) % size) for i in range(size)]
     down = [(j, i) for i, j in up]
-    last = lax.slice_in_dim(array, length - width, length, axis=dim)
-    initial = lax.slice_in_dim(array, 0, width, axis=dim)
+    last = velocity[1, :, length - width :, :]
+    initial = velocity[1, :, :width, :]
     before = lax.ppermute(last, axes, up)
     after = lax.ppermute(initial, axes, down)
-    return jnp.concatenate([before, array, after], axis=dim)
+    return before, after
 
 
 def factor_kernel(gram_ref, upper_ref, inverse_ref, rest_ref, ops_ref):
@@ -137,9 +137,10 @@
         row_count = velocity.shape[2]
         col_count = velocity.shape[3]
         total_cells = row_count * total * col_count
+        before, after = halo(velocity, AXES, total, 2)
         comp_u = velocity[0]
         comp_v = velocity[1]
-        padded = extended(comp_v, AXES, total, 1, 2)
+        padded = jnp.concatenate([before, comp_v, after], axis=1)
         u_second = lax.optimization_barrier(along_second(comp_u))
         v_first = stencil_rows(padded, row_count) / 12.0
         vorticity = v_first - u_second

time: 111 us -> 111 us (level)
    squeeze x0 -> x1, local copies, waits for them, and re-layouts: none -> 2.71 us  [halo(): initial = velocity[1, :, :width, :]]
    squeeze x1, local copies, waits for them, and re-layouts: 2.42 us -> 0.54 us  [local(): comp_v = velocity[1]]
    unnamed x2 -> x4, local copies, waits for them, and re-layouts: 2.43 us -> 2.44 us
  transfers between devices with their start and end apart: 3 -> 3, of which waited for: 3 -> 3; matrix products, arithmetic and copies ran while one was open for 5% -> 6% of each run, Pallas kernels for 0% -> 0%
where the time goes in v7:
time: 111 us; the launch traced here: 110 us
  blocking collectives  37.3 us (34%)
  waiting for transfers between devices  23.6 us (21%)
  Pallas kernels  14.9 us (13%)
  starting transfers between devices  13.8 us (12%)
  local copies, waits for them, and re-layouts  9.3 us (8%)
  other arithmetic  6.68 us (6%)
  matrix products  4.01 us (4%)
    all_to_all x3, blocking collectives, gather_sum(): gathered = lax.all_to_all(stacked, axes, 0, 0, tiled=True)  37.3 us
    pallas_call x1, Pallas kernels, factor(): pl.pallas_call(factor_kernel, out_shape=(jax.ShapeDtypeStruct((size, size...  14.9 us
    all_to_all x1, waiting for transfers between devices, gather_sum(): gathered = lax.all_to_all(stacked, axes, 0, 0, tiled=True)  13.5 us
    ppermute x1, waiting for transfers between devices, halo(): before = lax.ppermute(last, axes, up)  8.04 us
    ppermute x1, starting transfers between devices, halo(): after = lax.ppermute(initial, axes, down)  6.1 us
    all_to_all x1, starting transfers between devices, gather_sum(): gathered = lax.all_to_all(stacked, axes, 0, 0, tiled=True)  5.77 us
    sub x1, other arithmetic, local(): vorticity = v_first - u_second  2.87 us
    div x1, other arithmetic, along_second(): (8.0 * (jnp.roll(field, -1, 2) - jnp.roll(field, 1, 2)) - (jnp.roll(field...  2.77 us
  transfers between devices with their start and end apart: 3, of which 3 were waited for; matrix products, arithmetic and copies ran while one was open for 6% of the time, Pallas kernels for 0%

profile of v7, /device:TPU:32, one launch (start us, length us, event | category | flops | bytes accessed | tf_op | source)
XLA Modules:
  0.0 110.3 jit_solution(16851927401988228746)
XLA Ops:
  0.6 0.0 copy-start
  0.6 2.7 %slice_bitcast_fusion.3 = (f32[128,2,768]{2,1,0:T(2,128)S(1)}, f32[128,2,768]{2,1,0:T(2,128)S(1)}) fusion(f32[2,128,4,768]{3,2,1,0:T(4,128)} %param.1), kind=kLoop, calls=%fused_computation.26 | loop fusion | bytes 3145728 | tf_op jit(solution)/shard_map/squeeze | solution.py:24
  3.4 6.1 %collective-permute-start = (f32[128,2,768]{2,1,0:T(2,128)S(1)}, f32[128,2,768]{2,1,0:T(2,128)S(1)}, u32[]{:S(2)}, u32[]{:S(2)}) collective-permute-start(f32[128,2,768]{2,1,0:T(2,128)S(1)} %get-tuple-element.8), channel_id=1, source_target_pairs={{1,0},{2,1},{3,2},{4,3},{5,4},{6,5},{7,6},{8,7},{9,8},{10,9},{11,1... | collective-permute-start | bytes 2359304 | tf_op jit(solution)/shard_map/ppermute | solution.py:26
  9.5 1.9 %collective-permute-start.1 = (f32[128,2,768]{2,1,0:T(2,128)S(1)}, f32[128,2,768]{2,1,0:T(2,128)S(1)}, u32[]{:S(2)}, u32[]{:S(2)}) collective-permute-start(f32[128,2,768]{2,1,0:T(2,128)S(1)} %get-tuple-element.9), channel_id=1, source_target_pairs={{0,1},{1,2},{2,3},{3,4},{4,5},{5,6},{6,7},{7,8},{8,9},{9,10},{10,1... | collective-permute-start | bytes 2359304 | tf_op jit(solution)/shard_map/ppermute | solution.py:25
  11.4 0.0 copy-done
  11.4 0.5 slice_bitcast_fusion.1
  11.9 0.9 fusion.33
  12.9 0.2 fusion.32
  13.1 0.2 fusion.34
  13.3 0.9 fusion.35
  14.2 2.8 %fusion.10 = f32[128,4,768]{2,1,0:T(4,128)S(1)} fusion(f32[128,4,1]{2,1,0:T(4,128)S(1)} %get-tuple-element.17, f32[128,4,767]{2,1,0:T(4,128)S(1)} %get-tuple-element.19, f32[128,4,767]{2,1,0:T(4,128)S(1)} %get-tuple-element.18, f32[128,4,1]{2,1,0:T(4,128)S(1)} %get-tuple-element.16, f32[128,4,2]{2,1,0:T(4,128)S(1)} %get-tuple-element.13, ...), kind=kLoop, calls=%fused_computation.17 | loop fusion | flops 3538944 | bytes 7864320 | tf_op jit(solution)/shard_map/div | solution.py:120
  16.9 2.0 %collective-permute-done = f32[128,2,768]{2,1,0:T(2,128)S(1)} collective-permute-done((f32[128,2,768]{2,1,0:T(2,128)S(1)}, f32[128,2,768]{2,1,0:T(2,128)S(1)}, u32[]{:S(2)}, u32[]{:S(2)}) %collective-permute-start) | collective-permute-done | bytes 786464 | tf_op jit(solution)/shard_map/ppermute | solution.py:26
  18.9 8.0 %collective-permute-done.1 = f32[128,2,768]{2,1,0:T(2,128)S(1)} collective-permute-done((f32[128,2,768]{2,1,0:T(2,128)S(1)}, f32[128,2,768]{2,1,0:T(2,128)S(1)}, u32[]{:S(2)}, u32[]{:S(2)}) %collective-permute-start.1) | collective-permute-done | bytes 786464 | tf_op jit(solution)/shard_map/ppermute | solution.py:25
  27.0 2.9 %fusion.5 = f32[128,4,768]{2,1,0:T(4,128)S(1)} fusion(f32[128,4,768]{2,1,0:T(4,128)S(1)} %fusion.10, f32[128,2,768]{2,1,0:T(2,128)S(1)} %collective-permute-done.1, f32[128,4,768]{2,1,0:T(4,128)S(1)} %get-tuple-element.10, f32[128,2,768]{2,1,0:T(2,128)S(1)} %collective-permute-done), kind=kLoop, calls=%fused_computation.9 | loop fusion | flops 3932160 | bytes 6291456 | tf_op jit(solution)/shard_map/sub | solution.py:146
  29.9 1.7 %fusion.16 = f32[128,128]{1,0:T(8,128)S(1)} fusion(f32[128,4,768]{2,1,0:T(4,128)S(1)} %fusion.5), kind=kOutput, calls=%fused_computation.24 | convolution fusion | flops 603996160 | bytes 1638400 | tf_op jit(solution)/shard_map/dot_general | solution.py:149
  31.6 0.1 fusion.36
  31.7 0.1 select_maximum_fusion
  31.8 10.3 %all_to_all.20 = f32[8,65,128]{2,1,0:T(8,128)S(1)} all-to-all(f32[8,65,128]{2,1,0:T(8,128)S(1)} %broadcast_in_dim.50), channel_id=1, replica_groups=mesh['zh'=4,'zl'=4,'y'=4,'x'=4,'core'=2] {'x','core'}, dimensions={0} | all-to-all | bytes 532480 | tf_op jit(solution)/shard_map/all_to_all | solution.py:106
  42.1 8.4 %all_to_all.21 = f32[4,65,128]{2,1,0:T(8,128)S(1)} all-to-all(f32[4,65,128]{2,1,0:T(8,128)S(1)} %broadcast_in_dim.52), channel_id=1, replica_groups=mesh['zh'=4,'zl'=4,'y'=4,'x'=4,'core'=2] {'y'}, dimensions={0} | all-to-all | bytes 266240 | tf_op jit(solution)/shard_map/all_to_all | solution.py:106
  50.5 18.6 %all_to_all.22 = f32[4,65,128]{2,1,0:T(8,128)S(1)} all-to-all(f32[4,65,128]{2,1,0:T(8,128)S(1)} %broadcast_in_dim.54), channel_id=1, replica_groups=mesh['zh'=4,'zl'=4,'y'=4,'x'=4,'core'=2] {'zl'}, dimensions={0} | all-to-all | bytes 266240 | tf_op jit(solution)/shard_map/all_to_all | solution.py:106
  69.1 0.7 broadcast_in_dim.56
  69.8 5.8 %all-to-all-start.3 = ((f32[4,65,128]{2,1,0:T(8,128)}), f32[4,65,128]{2,1,0:T(8,128)S(1)}, u32[]{:S(2)}, u32[]{:S(2)}) async-start(f32[4,65,128]{2,1,0:T(8,128)} %broadcast_in_dim.56), calls=%async_computation.3 | async-start | bytes 294912 | tf_op jit(solution)/shard_map/all_to_all | solution.py:106
  75.6 0.3 copy.9
  75.9 0.5 copy.7
  76.3 13.5 %all-to-all-done.3 = f32[4,65,128]{2,1,0:T(8,128)S(1)} async-done(((f32[4,65,128]{2,1,0:T(8,128)}), f32[4,65,128]{2,1,0:T(8,128)S(1)}, u32[]{:S(2)}, u32[]{:S(2)}) %all-to-all-start.3) | async-done | bytes 133152 | tf_op jit(solution)/shard_map/all_to_all | solution.py:106
  89.9 0.1 slice.215
  89.9 0.1 copy.5
  90.0 0.1 bitcast_select_fusion.1
  90.1 0.1 copy.6
  90.2 0.7 maximum_maximum_fusion.gram_ref
  90.9 14.9 %shard_map.30 = (f32[128,128]{1,0:T(8,128)}, f32[128,128]{1,0:T(8,128)}) custom-call(f32[128,128]{1,0:T(8,128)} %maximum_maximum_fusion.gram_ref), custom_call_target="tpu_custom_call" | custom-call | tf_op jit(solution)/shard_map/pallas_call | solution.py:61
  105.8 2.3 %fusion.19 = f32[128,4,768]{2,0,1:T(8,128)S(1)} fusion(f32[4,768,128]{2,1,0:T(8,128)S(1)} %bitcast.40, f32[128,128]{1,0:T(8,128)} %get-tuple-element.4), kind=kOutput, calls=%fused_computation.28 | convolution fusion | flops 603979776 | bytes 3211264 | tf_op jit(solution)/shard_map/dot_general | solution.py:164
  108.2 2.2 %copy.8 = f32[128,4,768]{2,1,0:T(4,128)} copy(f32[128,4,768]{2,0,1:T(8,128)S(1)} %fusion.19) | data formatting | bytes 3145728
  (8 shorter events, 0.1 us)
Async XLA Ops:
  0.6 10.8 %copy-start = (f32[2,128,4,768]{3,2,1,0:T(4,128)S(1)}, f32[2,128,4,768]{3,2,1,0:T(4,128)}, u32[]{:S(2)}) copy-start(f32[2,128,4,768]{3,2,1,0:T(4,128)} %param.1) | copy-start | bytes 9437188
  3.4 15.6 %collective-permute-start = (f32[128,2,768]{2,1,0:T(2,128)S(1)}, f32[128,2,768]{2,1,0:T(2,128)S(1)}, u32[]{:S(2)}, u32[]{:S(2)}) collective-permute-start(f32[128,2,768]{2,1,0:T(2,128)S(1)} %get-tuple-element.8), channel_id=1, source_target_pairs={{1,0},{2,1},{3,2},{4,3},{5,4},{6,5},{7,6},{8,7},{9,8},{10,9},{11,1... | collective-permute-start | bytes 2359304 | tf_op jit(solution)/shard_map/ppermute | solution.py:26
  9.5 17.5 %collective-permute-start.1 = (f32[128,2,768]{2,1,0:T(2,128)S(1)}, f32[128,2,768]{2,1,0:T(2,128)S(1)}, u32[]{:S(2)}, u32[]{:S(2)}) collective-permute-start(f32[128,2,768]{2,1,0:T(2,128)S(1)} %get-tuple-element.9), channel_id=1, source_target_pairs={{0,1},{1,2},{2,3},{3,4},{4,5},{5,6},{6,7},{7,8},{8,9},{9,10},{10,1... | collective-permute-start | bytes 2359304 | tf_op jit(solution)/shard_map/ppermute | solution.py:25
  69.8 20.0 %all-to-all-start.3 = ((f32[4,65,128]{2,1,0:T(8,128)}), f32[4,65,128]{2,1,0:T(8,128)S(1)}, u32[]{:S(2)}, u32[]{:S(2)}) async-start(f32[4,65,128]{2,1,0:T(8,128)} %broadcast_in_dim.56), calls=%async_computation.3 | async-start | bytes 294912 | tf_op jit(solution)/shard_map/all_to_all | solution.py:106

commit v8 on v6

--- a/solution.py
+++ b/solution.py
@@ -6,7 +6,7 @@
 from jax.sharding import Mesh
 from jax.sharding import PartitionSpec as P
 
-AXES = ("zh", "zl", "y", "x", "core")
+AXES = ("z3", "z21", "z0", "y", "x", "core")
 
 
 def ring_index(shape):
@@ -155,9 +155,9 @@
         )
         gram = pack_symmetric(local_gram)
         gram = gather_sum(gram, ("x", "core"), sizes["x"] * sizes["core"])
-        gram = gather_sum(gram, ("y",), sizes["y"])
-        gram = gather_sum(gram, ("zl",), sizes["zl"])
-        gram = gather_sum(gram, ("zh",), sizes["zh"])
+        gram = gather_sum(gram, ("z0", "y"), sizes["z0"] * sizes["y"])
+        gram = gather_sum(gram, ("z21",), sizes["z21"])
+        gram = gather_sum(gram, ("z3",), sizes["z3"])
         gram = unpack_symmetric(gram)
         upper, inverse_lower = factor(gram)
         spatial_modes = jnp.dot(
@@ -178,10 +178,11 @@
     x_size = 4 if count % (core * 4) == 0 else 1
     y_size = 4 if count % (core * x_size * 4) == 0 else 1
     rest = count // (core * x_size * y_size)
-    zl = 4 if rest % 4 == 0 else rest
-    zh = rest // zl
-    sizes = {"zh": zh, "zl": zl, "y": y_size, "x": x_size, "core": core}
-    view = Mesh(devices.reshape(zh, zl, y_size, x_size, core), AXES)
+    z0 = 2 if rest % 2 == 0 else 1
+    z21 = 4 if rest % (z0 * 4) == 0 else 1
+    z3 = rest // (z0 * z21)
+    sizes = {"z3": z3, "z21": z21, "z0": z0, "y": y_size, "x": x_size, "core": core}
+    view = Mesh(devices.reshape(z3, z21, z0, y_size, x_size, core), AXES)
     return jax.shard_map(
         make_local(sizes),
         mesh=view,

time: 111 us -> 121 us (1.090)
  blocking collectives: 37.3 us -> 43.5 us
  starting transfers between devices: 13.8 us -> 18 us
    all_to_all x3, blocking collectives: 37.3 us -> 43.5 us  [gather_sum(): gathered = lax.all_to_all(stacked, axes, 0, 0, tiled=True)]
    all_to_all x1, starting transfers between devices: 5.77 us -> 9.94 us  [gather_sum(): gathered = lax.all_to_all(stacked, axes, 0, 0, tiled=True)]
where the time goes in v8:
time: 121 us; the launch traced here: 120 us
  blocking collectives  43.5 us (36%)
  waiting for transfers between devices  23.5 us (19%)
  starting transfers between devices  18 us (15%)
  Pallas kernels  14.9 us (12%)
  local copies, waits for them, and re-layouts  9.05 us (7%)
  other arithmetic  6.68 us (6%)
  matrix products  4.01 us (3%)
    all_to_all x3, blocking collectives, gather_sum(): gathered = lax.all_to_all(stacked, axes, 0, 0, tiled=True)  43.5 us
    pallas_call x1, Pallas kernels, factor(): pl.pallas_call(factor_kernel, out_shape=(jax.ShapeDtypeStruct((size, size...  14.9 us
    all_to_all x1, waiting for transfers between devices, gather_sum(): gathered = lax.all_to_all(stacked, axes, 0, 0, tiled=True)  12.9 us
    all_to_all x1, starting transfers between devices, gather_sum(): gathered = lax.all_to_all(stacked, axes, 0, 0, tiled=True)  9.94 us
    ppermute x1, waiting for transfers between devices, extended(): before = lax.ppermute(last, axes, up)  8.04 us
    ppermute x1, starting transfers between devices, extended(): after = lax.ppermute(initial, axes, down)  6.1 us
    sub x1, other arithmetic, local(): vorticity = v_first - u_second  2.87 us
    div x1, other arithmetic, along_second(): (8.0 * (jnp.roll(field, -1, 2) - jnp.roll(field, 1, 2)) - (jnp.roll(field...  2.77 us
  transfers between devices with their start and end apart: 3, of which 3 were waited for; matrix products, arithmetic and copies ran while one was open for 5% of the time, Pallas kernels for 0%

profile of v8, /device:TPU:32, one launch (start us, length us, event | category | flops | bytes accessed | tf_op | source)
XLA Modules:
  0.0 120.4 jit_solution(12311517931787236554)
XLA Ops:
  0.6 2.4 %slice_bitcast_fusion.1 = (f32[128,4,768]{2,1,0:T(4,128)S(1)}, f32[128,4,768]{2,1,0:T(4,128)S(1)}) fusion(f32[2,128,4,768]{3,2,1,0:T(4,128)} %param.1), kind=kLoop, calls=%fused_computation.22 | loop fusion | bytes 6291456 | tf_op jit(solution)/shard_map/squeeze | solution.py:141
  3.1 0.6 fusion.33
  3.7 6.1 %collective-permute-start = (f32[128,2,768]{2,1,0:T(2,128)S(1)}, f32[128,2,768]{2,1,0:T(2,128)S(1)}, u32[]{:S(2)}, u32[]{:S(2)}) collective-permute-start(f32[128,2,768]{2,1,0:T(2,128)S(1)} %get-tuple-element.10), channel_id=1, source_target_pairs={{1,0},{2,1},{3,2},{4,3},{5,4},{6,5},{7,6},{8,7},{9,8},{10,9},{11,1... | collective-permute-start | bytes 2359304 | tf_op jit(solution)/shard_map/ppermute | solution.py:26
  9.8 1.9 %collective-permute-start.1 = (f32[128,2,768]{2,1,0:T(2,128)S(1)}, f32[128,2,768]{2,1,0:T(2,128)S(1)}, u32[]{:S(2)}, u32[]{:S(2)}) collective-permute-start(f32[128,2,768]{2,1,0:T(2,128)S(1)} %get-tuple-element.11), channel_id=1, source_target_pairs={{0,1},{1,2},{2,3},{3,4},{4,5},{5,6},{6,7},{7,8},{8,9},{9,10},{10,1... | collective-permute-start | bytes 2359304 | tf_op jit(solution)/shard_map/ppermute | solution.py:25
  11.7 0.9 fusion.35
  12.6 0.2 fusion.34
  12.8 0.2 fusion.36
  13.0 0.9 fusion.37
  13.9 2.8 %fusion.10 = f32[128,4,768]{2,1,0:T(4,128)S(1)} fusion(f32[128,4,1]{2,1,0:T(4,128)S(1)} %get-tuple-element.17, f32[128,4,767]{2,1,0:T(4,128)S(1)} %get-tuple-element.19, f32[128,4,767]{2,1,0:T(4,128)S(1)} %get-tuple-element.18, f32[128,4,1]{2,1,0:T(4,128)S(1)} %get-tuple-element.16, f32[128,4,2]{2,1,0:T(4,128)S(1)} %get-tuple-element.13, ...), kind=kLoop, calls=%fused_computation.17 | loop fusion | flops 3538944 | bytes 7864320 | tf_op jit(solution)/shard_map/div | solution.py:120
  16.7 2.6 %collective-permute-done = f32[128,2,768]{2,1,0:T(2,128)S(1)} collective-permute-done((f32[128,2,768]{2,1,0:T(2,128)S(1)}, f32[128,2,768]{2,1,0:T(2,128)S(1)}, u32[]{:S(2)}, u32[]{:S(2)}) %collective-permute-start) | collective-permute-done | bytes 786464 | tf_op jit(solution)/shard_map/ppermute | solution.py:26
  19.3 8.0 %collective-permute-done.1 = f32[128,2,768]{2,1,0:T(2,128)S(1)} collective-permute-done((f32[128,2,768]{2,1,0:T(2,128)S(1)}, f32[128,2,768]{2,1,0:T(2,128)S(1)}, u32[]{:S(2)}, u32[]{:S(2)}) %collective-permute-start.1) | collective-permute-done | bytes 786464 | tf_op jit(solution)/shard_map/ppermute | solution.py:25
  27.3 2.9 %fusion.5 = f32[128,4,768]{2,1,0:T(4,128)S(1)} fusion(f32[128,4,768]{2,1,0:T(4,128)S(1)} %fusion.10, f32[128,2,768]{2,1,0:T(2,128)S(1)} %collective-permute-done.1, f32[128,4,768]{2,1,0:T(4,128)S(1)} %get-tuple-element.8, f32[128,2,768]{2,1,0:T(2,128)S(1)} %collective-permute-done), kind=kLoop, calls=%fused_computation.9 | loop fusion | flops 3932160 | bytes 6291456 | tf_op jit(solution)/shard_map/sub | solution.py:145
  30.2 1.7 %fusion.16 = f32[128,128]{1,0:T(8,128)S(1)} fusion(f32[128,4,768]{2,1,0:T(4,128)S(1)} %fusion.5), kind=kOutput, calls=%fused_computation.24 | convolution fusion | flops 603996160 | bytes 1638400 | tf_op jit(solution)/shard_map/dot_general | solution.py:148
  31.9 0.1 fusion.38
  32.0 0.1 select_maximum_fusion
  32.1 10.3 %all_to_all.20 = f32[8,65,128]{2,1,0:T(8,128)S(1)} all-to-all(f32[8,65,128]{2,1,0:T(8,128)S(1)} %broadcast_in_dim.50), channel_id=1, replica_groups=mesh['z3'=2,'z21'=4,'z0'=2,'y'=4,'x'=4,'core'=2] {'x','core'}, dimensions={0} | all-to-all | bytes 532480 | tf_op jit(solution)/shard_map/all_to_all | solution.py:106
  42.4 20.1 %all_to_all.21 = f32[8,65,128]{2,1,0:T(8,128)S(1)} all-to-all(f32[8,65,128]{2,1,0:T(8,128)S(1)} %broadcast_in_dim.52), channel_id=1, replica_groups=mesh['z3'=2,'z21'=4,'z0'=2,'y'=4,'x'=4,'core'=2] {'z0','y'}, dimensions={0} | all-to-all | bytes 532480 | tf_op jit(solution)/shard_map/all_to_all | solution.py:106
  62.6 13.1 %all_to_all.22 = f32[4,65,128]{2,1,0:T(8,128)S(1)} all-to-all(f32[4,65,128]{2,1,0:T(8,128)S(1)} %broadcast_in_dim.54), channel_id=1, replica_groups=mesh['z3'=2,'z21'=4,'z0'=2,'y'=4,'x'=4,'core'=2] {'z21'}, dimensions={0} | all-to-all | bytes 266240 | tf_op jit(solution)/shard_map/all_to_all | solution.py:106
  75.7 0.6 broadcast_in_dim.56
  76.3 9.9 %all-to-all-start.3 = ((f32[2,65,128]{2,1,0:T(8,128)}), f32[2,65,128]{2,1,0:T(8,128)S(1)}, u32[]{:S(2)}, u32[]{:S(2)}) async-start(f32[2,65,128]{2,1,0:T(8,128)} %broadcast_in_dim.56), calls=%async_computation.3 | async-start | bytes 147456 | tf_op jit(solution)/shard_map/all_to_all | solution.py:106
  86.2 0.3 copy.9
  86.5 0.5 copy.7
  87.0 12.9 %all-to-all-done.3 = f32[2,65,128]{2,1,0:T(8,128)S(1)} async-done(((f32[2,65,128]{2,1,0:T(8,128)}), f32[2,65,128]{2,1,0:T(8,128)S(1)}, u32[]{:S(2)}, u32[]{:S(2)}) %all-to-all-start.3) | async-done | bytes 66592 | tf_op jit(solution)/shard_map/all_to_all | solution.py:106
  99.9 0.1 slice.227
  100.0 0.1 copy.5
  100.0 0.1 bitcast_select_fusion.1
  100.1 0.1 copy.6
  100.2 0.7 maximum_maximum_fusion.gram_ref
  100.9 14.9 %shard_map.30 = (f32[128,128]{1,0:T(8,128)}, f32[128,128]{1,0:T(8,128)}) custom-call(f32[128,128]{1,0:T(8,128)} %maximum_maximum_fusion.gram_ref), custom_call_target="tpu_custom_call" | custom-call | tf_op jit(solution)/shard_map/pallas_call | solution.py:61
  115.9 2.3 %fusion.19 = f32[128,4,768]{2,0,1:T(8,128)S(1)} fusion(f32[4,768,128]{2,1,0:T(8,128)S(1)} %bitcast.36, f32[128,128]{1,0:T(8,128)} %get-tuple-element.4), kind=kOutput, calls=%fused_computation.26 | convolution fusion | flops 603979776 | bytes 3211264 | tf_op jit(solution)/shard_map/dot_general | solution.py:163
  118.2 2.2 %copy.8 = f32[128,4,768]{2,1,0:T(4,128)} copy(f32[128,4,768]{2,0,1:T(8,128)S(1)} %fusion.19) | data formatting | bytes 3145728
  (8 shorter events, 0.1 us)
Async XLA Ops:
  3.7 15.6 %collective-permute-start = (f32[128,2,768]{2,1,0:T(2,128)S(1)}, f32[128,2,768]{2,1,0:T(2,128)S(1)}, u32[]{:S(2)}, u32[]{:S(2)}) collective-permute-start(f32[128,2,768]{2,1,0:T(2,128)S(1)} %get-tuple-element.10), channel_id=1, source_target_pairs={{1,0},{2,1},{3,2},{4,3},{5,4},{6,5},{7,6},{8,7},{9,8},{10,9},{11,1... | collective-permute-start | bytes 2359304 | tf_op jit(solution)/shard_map/ppermute | solution.py:26
  9.8 17.5 %collective-permute-start.1 = (f32[128,2,768]{2,1,0:T(2,128)S(1)}, f32[128,2,768]{2,1,0:T(2,128)S(1)}, u32[]{:S(2)}, u32[]{:S(2)}) collective-permute-start(f32[128,2,768]{2,1,0:T(2,128)S(1)} %get-tuple-element.11), channel_id=1, source_target_pairs={{0,1},{1,2},{2,3},{3,4},{4,5},{5,6},{6,7},{7,8},{8,9},{9,10},{10,1... | collective-permute-start | bytes 2359304 | tf_op jit(solution)/shard_map/ppermute | solution.py:25
  76.3 23.6 %all-to-all-start.3 = ((f32[2,65,128]{2,1,0:T(8,128)}), f32[2,65,128]{2,1,0:T(8,128)S(1)}, u32[]{:S(2)}, u32[]{:S(2)}) async-start(f32[2,65,128]{2,1,0:T(8,128)} %broadcast_in_dim.56), calls=%async_computation.3 | async-start | bytes 147456 | tf_op jit(solution)/shard_map/all_to_all | solution.py:106

commit v9 on v6

--- a/solution.py
+++ b/solution.py
@@ -154,10 +154,10 @@
             / total_cells
         )
         gram = pack_symmetric(local_gram)
+        gram = gather_sum(gram, ("zh",), sizes["zh"])
+        gram = gather_sum(gram, ("zl",), sizes["zl"])
+        gram = gather_sum(gram, ("y",), sizes["y"])
         gram = gather_sum(gram, ("x", "core"), sizes["x"] * sizes["core"])
-        gram = gather_sum(gram, ("y",), sizes["y"])
-        gram = gather_sum(gram, ("zl",), sizes["zl"])
-        gram = gather_sum(gram, ("zh",), sizes["zh"])
         gram = unpack_symmetric(gram)
         upper, inverse_lower = factor(gram)
         spatial_modes = jnp.dot(

time: 111 us -> 114 us (1.027)
  the two profiles are of different devices: /device:TPU:32 before, /device:TPU:1 now
where the time goes in v9:
time: 114 us; the launch traced here: 113 us
  blocking collectives  40.3 us (35%)
  starting transfers between devices  26.2 us (23%)
  Pallas kernels  14.9 us (13%)
  waiting for transfers between devices  11 us (10%)
  local copies, waits for them, and re-layouts  9.13 us (8%)
  other arithmetic  6.68 us (6%)
  matrix products  4.01 us (4%)
    all_to_all x3, blocking collectives, gather_sum(): gathered = lax.all_to_all(stacked, axes, 0, 0, tiled=True)  40.3 us
    all_to_all x1, starting transfers between devices, gather_sum(): gathered = lax.all_to_all(stacked, axes, 0, 0, tiled=True)  15.5 us
    pallas_call x1, Pallas kernels, factor(): pl.pallas_call(factor_kernel, out_shape=(jax.ShapeDtypeStruct((size, size...  14.9 us
    ppermute x1, starting transfers between devices, extended(): after = lax.ppermute(initial, axes, down)  8.79 us
    all_to_all x1, waiting for transfers between devices, gather_sum(): gathered = lax.all_to_all(stacked, axes, 0, 0, tiled=True)  6.08 us
    ppermute x1, waiting for transfers between devices, extended(): before = lax.ppermute(last, axes, up)  4.95 us
    sub x1, other arithmetic, local(): vorticity = v_first - u_second  2.87 us
    div x1, other arithmetic, along_second(): (8.0 * (jnp.roll(field, -1, 2) - jnp.roll(field, 1, 2)) - (jnp.roll(field...  2.77 us
  transfers between devices with their start and end apart: 3, of which 2 were waited for; matrix products, arithmetic and copies ran while one was open for 5% of the time, Pallas kernels for 0%

profile of v9, /device:TPU:1, one launch (start us, length us, event | category | flops | bytes accessed | tf_op | source)
XLA Modules:
  0.0 113.1 jit_solution(16600081607537523088)
XLA Ops:
  0.6 2.4 %slice_bitcast_fusion.1 = (f32[128,4,768]{2,1,0:T(4,128)S(1)}, f32[128,4,768]{2,1,0:T(4,128)S(1)}) fusion(f32[2,128,4,768]{3,2,1,0:T(4,128)} %param.1), kind=kLoop, calls=%fused_computation.22 | loop fusion | bytes 6291456 | tf_op jit(solution)/shard_map/squeeze | solution.py:141
  3.1 0.6 fusion.32
  3.7 8.8 %collective-permute-start = (f32[128,2,768]{2,1,0:T(2,128)S(1)}, f32[128,2,768]{2,1,0:T(2,128)S(1)}, u32[]{:S(2)}, u32[]{:S(2)}) collective-permute-start(f32[128,2,768]{2,1,0:T(2,128)S(1)} %get-tuple-element.10), channel_id=1, source_target_pairs={{1,0},{2,1},{3,2},{4,3},{5,4},{6,5},{7,6},{8,7},{9,8},{10,9},{11,1... | collective-permute-start | bytes 2359304 | tf_op jit(solution)/shard_map/ppermute | solution.py:26
  12.5 1.9 %collective-permute-start.1 = (f32[128,2,768]{2,1,0:T(2,128)S(1)}, f32[128,2,768]{2,1,0:T(2,128)S(1)}, u32[]{:S(2)}, u32[]{:S(2)}) collective-permute-start(f32[128,2,768]{2,1,0:T(2,128)S(1)} %get-tuple-element.11), channel_id=1, source_target_pairs={{0,1},{1,2},{2,3},{3,4},{4,5},{5,6},{6,7},{7,8},{8,9},{9,10},{10,1... | collective-permute-start | bytes 2359304 | tf_op jit(solution)/shard_map/ppermute | solution.py:25
  14.4 0.9 fusion.34
  15.3 0.2 fusion.33
  15.5 0.2 fusion.35
  15.7 0.9 fusion.36
  16.6 2.8 %fusion.10 = f32[128,4,768]{2,1,0:T(4,128)S(1)} fusion(f32[128,4,1]{2,1,0:T(4,128)S(1)} %get-tuple-element.17, f32[128,4,767]{2,1,0:T(4,128)S(1)} %get-tuple-element.19, f32[128,4,767]{2,1,0:T(4,128)S(1)} %get-tuple-element.18, f32[128,4,1]{2,1,0:T(4,128)S(1)} %get-tuple-element.16, f32[128,4,2]{2,1,0:T(4,128)S(1)} %get-tuple-element.13, ...), kind=kLoop, calls=%fused_computation.17 | loop fusion | flops 3538944 | bytes 7864320 | tf_op jit(solution)/shard_map/div | solution.py:120
  19.4 0.0 collective-permute-done
  19.4 4.9 %collective-permute-done.1 = f32[128,2,768]{2,1,0:T(2,128)S(1)} collective-permute-done((f32[128,2,768]{2,1,0:T(2,128)S(1)}, f32[128,2,768]{2,1,0:T(2,128)S(1)}, u32[]{:S(2)}, u32[]{:S(2)}) %collective-permute-start.1) | collective-permute-done | bytes 786464 | tf_op jit(solution)/shard_map/ppermute | solution.py:25
  24.4 2.9 %fusion.5 = f32[128,4,768]{2,1,0:T(4,128)S(1)} fusion(f32[128,4,768]{2,1,0:T(4,128)S(1)} %fusion.10, f32[128,2,768]{2,1,0:T(2,128)S(1)} %collective-permute-done.1, f32[128,4,768]{2,1,0:T(4,128)S(1)} %get-tuple-element.8, f32[128,2,768]{2,1,0:T(2,128)S(1)} %collective-permute-done), kind=kLoop, calls=%fused_computation.9 | loop fusion | flops 3932160 | bytes 6291456 | tf_op jit(solution)/shard_map/sub | solution.py:145
  27.2 1.7 %fusion.16 = f32[128,128]{1,0:T(8,128)S(1)} fusion(f32[128,4,768]{2,1,0:T(4,128)S(1)} %fusion.5), kind=kOutput, calls=%fused_computation.24 | convolution fusion | flops 603996160 | bytes 1638400 | tf_op jit(solution)/shard_map/dot_general | solution.py:148
  28.9 0.1 fusion.37
  29.0 0.1 select_maximum_fusion
  29.1 22.0 %all_to_all.20 = f32[4,65,128]{2,1,0:T(8,128)S(1)} all-to-all(f32[4,65,128]{2,1,0:T(8,128)S(1)} %broadcast_in_dim.50), channel_id=1, replica_groups=mesh['zh'=4,'zl'=4,'y'=4,'x'=4,'core'=2] {'zh'}, dimensions={0} | all-to-all | bytes 266240 | tf_op jit(solution)/shard_map/all_to_all | solution.py:106
  51.2 9.8 %all_to_all.21 = f32[4,65,128]{2,1,0:T(8,128)S(1)} all-to-all(f32[4,65,128]{2,1,0:T(8,128)S(1)} %broadcast_in_dim.52), channel_id=1, replica_groups=mesh['zh'=4,'zl'=4,'y'=4,'x'=4,'core'=2] {'zl'}, dimensions={0} | all-to-all | bytes 266240 | tf_op jit(solution)/shard_map/all_to_all | solution.py:106
  61.0 8.5 %all_to_all.22 = f32[4,65,128]{2,1,0:T(8,128)S(1)} all-to-all(f32[4,65,128]{2,1,0:T(8,128)S(1)} %broadcast_in_dim.54), channel_id=1, replica_groups=mesh['zh'=4,'zl'=4,'y'=4,'x'=4,'core'=2] {'y'}, dimensions={0} | all-to-all | bytes 266240 | tf_op jit(solution)/shard_map/all_to_all | solution.py:106
  69.5 0.7 broadcast_in_dim.56
  70.3 15.5 %all-to-all-start.3 = ((f32[8,65,128]{2,1,0:T(8,128)}), f32[8,65,128]{2,1,0:T(8,128)S(1)}, u32[]{:S(2)}, u32[]{:S(2)}) async-start(f32[8,65,128]{2,1,0:T(8,128)} %broadcast_in_dim.56), calls=%async_computation.3 | async-start | bytes 589824 | tf_op jit(solution)/shard_map/all_to_all | solution.py:106
  85.8 0.3 copy.9
  86.1 0.5 copy.7
  86.5 6.1 %all-to-all-done.3 = f32[8,65,128]{2,1,0:T(8,128)S(1)} async-done(((f32[8,65,128]{2,1,0:T(8,128)}), f32[8,65,128]{2,1,0:T(8,128)S(1)}, u32[]{:S(2)}, u32[]{:S(2)}) %all-to-all-start.3) | async-done | bytes 266272 | tf_op jit(solution)/shard_map/all_to_all | solution.py:106
  92.7 0.1 slice.217
  92.7 0.1 copy.5
  92.8 0.1 bitcast_select_fusion.1
  92.9 0.1 copy.6
  93.0 0.7 maximum_maximum_fusion.gram_ref
  93.7 14.9 %shard_map.30 = (f32[128,128]{1,0:T(8,128)}, f32[128,128]{1,0:T(8,128)}) custom-call(f32[128,128]{1,0:T(8,128)} %maximum_maximum_fusion.gram_ref), custom_call_target="tpu_custom_call" | custom-call | tf_op jit(solution)/shard_map/pallas_call | solution.py:61
  108.6 2.3 %fusion.19 = f32[128,4,768]{2,0,1:T(8,128)S(1)} fusion(f32[4,768,128]{2,1,0:T(8,128)S(1)} %bitcast.36, f32[128,128]{1,0:T(8,128)} %get-tuple-element.4), kind=kOutput, calls=%fused_computation.26 | convolution fusion | flops 603979776 | bytes 3211264 | tf_op jit(solution)/shard_map/dot_general | solution.py:163
  111.0 2.2 %copy.8 = f32[128,4,768]{2,1,0:T(4,128)} copy(f32[128,4,768]{2,0,1:T(8,128)S(1)} %fusion.19) | data formatting | bytes 3145728
  (8 shorter events, 0.1 us)
Async XLA Ops:
  3.7 15.7 %collective-permute-start = (f32[128,2,768]{2,1,0:T(2,128)S(1)}, f32[128,2,768]{2,1,0:T(2,128)S(1)}, u32[]{:S(2)}, u32[]{:S(2)}) collective-permute-start(f32[128,2,768]{2,1,0:T(2,128)S(1)} %get-tuple-element.10), channel_id=1, source_target_pairs={{1,0},{2,1},{3,2},{4,3},{5,4},{6,5},{7,6},{8,7},{9,8},{10,9},{11,1... | collective-permute-start | bytes 2359304 | tf_op jit(solution)/shard_map/ppermute | solution.py:26
  12.5 11.9 %collective-permute-start.1 = (f32[128,2,768]{2,1,0:T(2,128)S(1)}, f32[128,2,768]{2,1,0:T(2,128)S(1)}, u32[]{:S(2)}, u32[]{:S(2)}) collective-permute-start(f32[128,2,768]{2,1,0:T(2,128)S(1)} %get-tuple-element.11), channel_id=1, source_target_pairs={{0,1},{1,2},{2,3},{3,4},{4,5},{5,6},{6,7},{7,8},{8,9},{9,10},{10,1... | collective-permute-start | bytes 2359304 | tf_op jit(solution)/shard_map/ppermute | solution.py:25
  70.3 22.4 %all-to-all-start.3 = ((f32[8,65,128]{2,1,0:T(8,128)}), f32[8,65,128]{2,1,0:T(8,128)S(1)}, u32[]{:S(2)}, u32[]{:S(2)}) async-start(f32[8,65,128]{2,1,0:T(8,128)} %broadcast_in_dim.56), calls=%async_computation.3 | async-start | bytes 589824 | tf_op jit(solution)/shard_map/all_to_all | solution.py:106

commit v10 on v6

--- a/solution.py
+++ b/solution.py
@@ -140,9 +140,11 @@
         comp_u = velocity[0]
         comp_v = velocity[1]
         padded = extended(comp_v, AXES, total, 1, 2)
-        u_second = lax.optimization_barrier(along_second(comp_u))
-        v_first = stencil_rows(padded, row_count) / 12.0
-        vorticity = v_first - u_second
+        edge = jnp.zeros_like(padded[:, :2])
+        inner = jnp.concatenate([edge, comp_v, edge], axis=1)
+        outer = jnp.concatenate([padded[:, :2], jnp.zeros_like(comp_v), padded[:, row_count + 2 :]], axis=1)
+        local_part = lax.optimization_barrier(stencil_rows(inner, row_count) / 12.0 - along_second(comp_u))
+        vorticity = local_part + stencil_rows(outer, row_count) / 12.0
         flattened = vorticity.reshape(snap_count, row_count * col_count)
         local_gram = (
             jnp.dot(

time: 111 us -> 110 us (level)
    div x1 -> x0, other arithmetic: 2.77 us -> none  [along_second(): (8.0 * (jnp.roll(field, -1, 2) - jnp.roll(field, 1, 2)) - (jnp.roll(field...]
    add x0 -> x1, other arithmetic: none -> 1.36 us  [local(): vorticity = local_part + stencil_rows(outer, row_count) / 12.0]
  transfers between devices with their start and end apart: 3 -> 3, of which waited for: 3 -> 3; matrix products, arithmetic and copies ran while one was open for 5% -> 6% of each run, Pallas kernels for 0% -> 0%
where the time goes in v10:
time: 110 us; the launch traced here: 109 us
  blocking collectives  37.5 us (34%)
  waiting for transfers between devices  23.2 us (21%)
  Pallas kernels  14.9 us (14%)
  starting transfers between devices  13.6 us (12%)
  local copies, waits for them, and re-layouts  9.07 us (8%)
  other arithmetic  6.1 us (6%)
  matrix products  4.01 us (4%)
    all_to_all x3, blocking collectives, gather_sum(): gathered = lax.all_to_all(stacked, axes, 0, 0, tiled=True)  37.5 us
    pallas_call x1, Pallas kernels, factor(): pl.pallas_call(factor_kernel, out_shape=(jax.ShapeDtypeStruct((size, size...  14.9 us
    all_to_all x1, waiting for transfers between devices, gather_sum(): gathered = lax.all_to_all(stacked, axes, 0, 0, tiled=True)  13.5 us
    ppermute x1, waiting for transfers between devices, extended(): before = lax.ppermute(last, axes, up)  8.04 us
    ppermute x1, starting transfers between devices, extended(): after = lax.ppermute(initial, axes, down)  6.1 us
    all_to_all x1, starting transfers between devices, gather_sum(): gathered = lax.all_to_all(stacked, axes, 0, 0, tiled=True)  5.56 us
    sub x1, other arithmetic, local(): stencil_rows(inner, row_count) / 12.0 - along_second(comp_u)  3.7 us
    unnamed x2, local copies, waits for them, and re-layouts  2.43 us
  transfers between devices with their start and end apart: 3, of which 3 were waited for; matrix products, arithmetic and copies ran while one was open for 6% of the time, Pallas kernels for 0%

profile of v10, /device:TPU:32, one launch (start us, length us, event | category | flops | bytes accessed | tf_op | source)
XLA Modules:
  0.0 109.1 jit_solution(6287028999230527832)
XLA Ops:
  0.6 2.4 %slice_bitcast_fusion = (f32[128,4,768]{2,1,0:T(4,128)S(1)}, f32[128,4,768]{2,1,0:T(4,128)S(1)}) fusion(f32[2,128,4,768]{3,2,1,0:T(4,128)} %param.1), kind=kLoop, calls=%fused_computation.27 | loop fusion | bytes 6291456 | tf_op jit(solution)/shard_map/squeeze | solution.py:140
  3.1 0.6 fusion.36
  3.7 6.1 %collective-permute-start = (f32[128,2,768]{2,1,0:T(2,128)S(1)}, f32[128,2,768]{2,1,0:T(2,128)S(1)}, u32[]{:S(2)}, u32[]{:S(2)}) collective-permute-start(f32[128,2,768]{2,1,0:T(2,128)S(1)} %get-tuple-element.11), channel_id=1, source_target_pairs={{1,0},{2,1},{3,2},{4,3},{5,4},{6,5},{7,6},{8,7},{9,8},{10,9},{11,1... | collective-permute-start | bytes 2359304 | tf_op jit(solution)/shard_map/ppermute | solution.py:26
  9.8 1.9 %collective-permute-start.1 = (f32[128,2,768]{2,1,0:T(2,128)S(1)}, f32[128,2,768]{2,1,0:T(2,128)S(1)}, u32[]{:S(2)}, u32[]{:S(2)}) collective-permute-start(f32[128,2,768]{2,1,0:T(2,128)S(1)} %get-tuple-element.10), channel_id=1, source_target_pairs={{0,1},{1,2},{2,3},{3,4},{4,5},{5,6},{6,7},{7,8},{8,9},{9,10},{10,1... | collective-permute-start | bytes 2359304 | tf_op jit(solution)/shard_map/ppermute | solution.py:25
  11.7 0.9 fusion.38
  12.6 0.9 fusion.40
  13.5 0.2 fusion.37
  13.7 0.2 fusion.39
  13.9 3.7 %fusion.4 = f32[128,4,768]{2,1,0:T(4,128)S(1)} fusion(f32[128,4,768]{2,1,0:T(4,128)S(1)} %get-tuple-element.9, f32[128,4,1]{2,1,0:T(4,128)S(1)} %get-tuple-element.17, f32[128,4,767]{2,1,0:T(4,128)S(1)} %get-tuple-element.19, f32[128,4,767]{2,1,0:T(4,128)S(1)} %get-tuple-element.18, f32[128,4,1]{2,1,0:T(4,128)S(1)} %get-tuple-element.16, ...), kind=kLoop, calls=%fused_computation.12 | loop fusion | flops 5898240 | bytes 9437184 | tf_op jit(solution)/shard_map/sub | solution.py:146
  17.6 1.6 %collective-permute-done = f32[128,2,768]{2,1,0:T(2,128)S(1)} collective-permute-done((f32[128,2,768]{2,1,0:T(2,128)S(1)}, f32[128,2,768]{2,1,0:T(2,128)S(1)}, u32[]{:S(2)}, u32[]{:S(2)}) %collective-permute-start) | collective-permute-done | bytes 786464 | tf_op jit(solution)/shard_map/ppermute | solution.py:26
  19.3 8.0 %collective-permute-done.1 = f32[128,2,768]{2,1,0:T(2,128)S(1)} collective-permute-done((f32[128,2,768]{2,1,0:T(2,128)S(1)}, f32[128,2,768]{2,1,0:T(2,128)S(1)}, u32[]{:S(2)}, u32[]{:S(2)}) %collective-permute-start.1) | collective-permute-done | bytes 786464 | tf_op jit(solution)/shard_map/ppermute | solution.py:25
  27.3 1.4 %fusion.10 = f32[128,4,768]{2,1,0:T(4,128)S(1)} fusion(f32[128,4,768]{2,1,0:T(4,128)S(1)} %fusion.4, f32[128,2,768]{2,1,0:T(2,128)S(1)} %collective-permute-done, f32[128,2,768]{2,1,0:T(2,128)S(1)} %collective-permute-done.1), kind=kLoop, calls=%fused_computation.18 | loop fusion | flops 2359296 | bytes 4718592 | tf_op jit(solution)/shard_map/add | solution.py:147
  28.7 1.7 %fusion.20 = f32[128,128]{1,0:T(8,128)S(1)} fusion(f32[128,4,768]{2,1,0:T(4,128)S(1)} %fusion.10), kind=kOutput, calls=%fused_computation.30 | convolution fusion | flops 603996160 | bytes 1638400 | tf_op jit(solution)/shard_map/dot_general | solution.py:150
  30.4 0.1 fusion.41
  30.5 0.1 select_maximum_fusion
  30.6 10.3 %all_to_all.20 = f32[8,65,128]{2,1,0:T(8,128)S(1)} all-to-all(f32[8,65,128]{2,1,0:T(8,128)S(1)} %broadcast_in_dim.52), channel_id=1, replica_groups=mesh['zh'=4,'zl'=4,'y'=4,'x'=4,'core'=2] {'x','core'}, dimensions={0} | all-to-all | bytes 532480 | tf_op jit(solution)/shard_map/all_to_all | solution.py:106
  40.9 8.4 %all_to_all.21 = f32[4,65,128]{2,1,0:T(8,128)S(1)} all-to-all(f32[4,65,128]{2,1,0:T(8,128)S(1)} %broadcast_in_dim.54), channel_id=1, replica_groups=mesh['zh'=4,'zl'=4,'y'=4,'x'=4,'core'=2] {'y'}, dimensions={0} | all-to-all | bytes 266240 | tf_op jit(solution)/shard_map/all_to_all | solution.py:106
  49.3 18.8 %all_to_all.22 = f32[4,65,128]{2,1,0:T(8,128)S(1)} all-to-all(f32[4,65,128]{2,1,0:T(8,128)S(1)} %broadcast_in_dim.56), channel_id=1, replica_groups=mesh['zh'=4,'zl'=4,'y'=4,'x'=4,'core'=2] {'zl'}, dimensions={0} | all-to-all | bytes 266240 | tf_op jit(solution)/shard_map/all_to_all | solution.py:106
  68.2 0.7 broadcast_in_dim.58
  68.8 5.6 %all-to-all-start.3 = ((f32[4,65,128]{2,1,0:T(8,128)}), f32[4,65,128]{2,1,0:T(8,128)S(1)}, u32[]{:S(2)}, u32[]{:S(2)}) async-start(f32[4,65,128]{2,1,0:T(8,128)} %broadcast_in_dim.58), calls=%async_computation.3 | async-start | bytes 294912 | tf_op jit(solution)/shard_map/all_to_all | solution.py:106
  74.4 0.3 copy.9
  74.7 0.5 copy.7
  75.1 13.5 %all-to-all-done.3 = f32[4,65,128]{2,1,0:T(8,128)S(1)} async-done(((f32[4,65,128]{2,1,0:T(8,128)}), f32[4,65,128]{2,1,0:T(8,128)S(1)}, u32[]{:S(2)}, u32[]{:S(2)}) %all-to-all-start.3) | async-done | bytes 133152 | tf_op jit(solution)/shard_map/all_to_all | solution.py:106
  88.7 0.1 slice.233
  88.7 0.1 copy.5
  88.8 0.1 bitcast_select_fusion.1
  88.9 0.1 copy.6
  89.0 0.7 maximum_maximum_fusion.gram_ref
  89.7 14.9 %shard_map.30 = (f32[128,128]{1,0:T(8,128)}, f32[128,128]{1,0:T(8,128)}) custom-call(f32[128,128]{1,0:T(8,128)} %maximum_maximum_fusion.gram_ref), custom_call_target="tpu_custom_call" | custom-call | tf_op jit(solution)/shard_map/pallas_call | solution.py:61
  104.6 2.3 %fusion.23 = f32[128,4,768]{2,0,1:T(8,128)S(1)} fusion(f32[4,768,128]{2,1,0:T(8,128)S(1)} %bitcast.36, f32[128,128]{1,0:T(8,128)} %get-tuple-element.4), kind=kOutput, calls=%fused_computation.32 | convolution fusion | flops 603979776 | bytes 3211264 | tf_op jit(solution)/shard_map/dot_general | solution.py:165
  107.0 2.2 %copy.8 = f32[128,4,768]{2,1,0:T(4,128)} copy(f32[128,4,768]{2,0,1:T(8,128)S(1)} %fusion.23) | data formatting | bytes 3145728
  (8 shorter events, 0.1 us)
Async XLA Ops:
  3.7 15.6 %collective-permute-start = (f32[128,2,768]{2,1,0:T(2,128)S(1)}, f32[128,2,768]{2,1,0:T(2,128)S(1)}, u32[]{:S(2)}, u32[]{:S(2)}) collective-permute-start(f32[128,2,768]{2,1,0:T(2,128)S(1)} %get-tuple-element.11), channel_id=1, source_target_pairs={{1,0},{2,1},{3,2},{4,3},{5,4},{6,5},{7,6},{8,7},{9,8},{10,9},{11,1... | collective-permute-start | bytes 2359304 | tf_op jit(solution)/shard_map/ppermute | solution.py:26
  9.8 17.5 %collective-permute-start.1 = (f32[128,2,768]{2,1,0:T(2,128)S(1)}, f32[128,2,768]{2,1,0:T(2,128)S(1)}, u32[]{:S(2)}, u32[]{:S(2)}) collective-permute-start(f32[128,2,768]{2,1,0:T(2,128)S(1)} %get-tuple-element.10), channel_id=1, source_target_pairs={{0,1},{1,2},{2,3},{3,4},{4,5},{5,6},{6,7},{7,8},{8,9},{9,10},{10,1... | collective-permute-start | bytes 2359304 | tf_op jit(solution)/shard_map/ppermute | solution.py:25
  68.8 19.8 %all-to-all-start.3 = ((f32[4,65,128]{2,1,0:T(8,128)}), f32[4,65,128]{2,1,0:T(8,128)S(1)}, u32[]{:S(2)}, u32[]{:S(2)}) async-start(f32[4,65,128]{2,1,0:T(8,128)} %broadcast_in_dim.58), calls=%async_computation.3 | async-start | bytes 294912 | tf_op jit(solution)/shard_map/all_to_all | solution.py:106

commit v11 on v10

--- a/solution.py
+++ b/solution.py
@@ -52,7 +52,7 @@
         ops_ref[...] = ops_ref[...] - factor_col * inverse_row
         return carry
 
-    lax.fori_loop(0, size, step, 0, unroll=2)
+    lax.fori_loop(0, size, step, 0, unroll=4)
 
 
 def factor(gram):

time: 110 us -> 110 us (level)
  no operation moved by 1% of the time
where the time goes in v11:
time: 110 us; the launch traced here: 109 us
  blocking collectives  37.5 us (34%)
  waiting for transfers between devices  23.2 us (21%)
  Pallas kernels  14.9 us (14%)
  starting transfers between devices  13.6 us (12%)
  local copies, waits for them, and re-layouts  9.07 us (8%)
  other arithmetic  6.1 us (6%)
  matrix products  4.01 us (4%)
    all_to_all x3, blocking collectives, gather_sum(): gathered = lax.all_to_all(stacked, axes, 0, 0, tiled=True)  37.5 us
    pallas_call x1, Pallas kernels, factor(): pl.pallas_call(factor_kernel, out_shape=(jax.ShapeDtypeStruct((size, size...  14.9 us
    all_to_all x1, waiting for transfers between devices, gather_sum(): gathered = lax.all_to_all(stacked, axes, 0, 0, tiled=True)  13.5 us
    ppermute x1, waiting for transfers between devices, extended(): before = lax.ppermute(last, axes, up)  8.04 us
    ppermute x1, starting transfers between devices, extended(): after = lax.ppermute(initial, axes, down)  6.1 us
    all_to_all x1, starting transfers between devices, gather_sum(): gathered = lax.all_to_all(stacked, axes, 0, 0, tiled=True)  5.56 us
    sub x1, other arithmetic, local(): stencil_rows(inner, row_count) / 12.0 - along_second(comp_u)  3.7 us
    unnamed x2, local copies, waits for them, and re-layouts  2.43 us
  transfers between devices with their start and end apart: 3, of which 3 were waited for; matrix products, arithmetic and copies ran while one was open for 6% of the time, Pallas kernels for 0%

profile of v11, /device:TPU:32, one launch (start us, length us, event | category | flops | bytes accessed | tf_op | source)
XLA Modules:
  0.0 109.1 jit_solution(7887989978172295774)
XLA Ops:
  0.6 2.4 %slice_bitcast_fusion = (f32[128,4,768]{2,1,0:T(4,128)S(1)}, f32[128,4,768]{2,1,0:T(4,128)S(1)}) fusion(f32[2,128,4,768]{3,2,1,0:T(4,128)} %param.1), kind=kLoop, calls=%fused_computation.27 | loop fusion | bytes 6291456 | tf_op jit(solution)/shard_map/squeeze | solution.py:140
  3.1 0.6 fusion.36
  3.7 6.1 %collective-permute-start = (f32[128,2,768]{2,1,0:T(2,128)S(1)}, f32[128,2,768]{2,1,0:T(2,128)S(1)}, u32[]{:S(2)}, u32[]{:S(2)}) collective-permute-start(f32[128,2,768]{2,1,0:T(2,128)S(1)} %get-tuple-element.11), channel_id=1, source_target_pairs={{1,0},{2,1},{3,2},{4,3},{5,4},{6,5},{7,6},{8,7},{9,8},{10,9},{11,1... | collective-permute-start | bytes 2359304 | tf_op jit(solution)/shard_map/ppermute | solution.py:26
  9.8 1.9 %collective-permute-start.1 = (f32[128,2,768]{2,1,0:T(2,128)S(1)}, f32[128,2,768]{2,1,0:T(2,128)S(1)}, u32[]{:S(2)}, u32[]{:S(2)}) collective-permute-start(f32[128,2,768]{2,1,0:T(2,128)S(1)} %get-tuple-element.10), channel_id=1, source_target_pairs={{0,1},{1,2},{2,3},{3,4},{4,5},{5,6},{6,7},{7,8},{8,9},{9,10},{10,1... | collective-permute-start | bytes 2359304 | tf_op jit(solution)/shard_map/ppermute | solution.py:25
  11.7 0.9 fusion.38
  12.6 0.9 fusion.40
  13.5 0.2 fusion.37
  13.7 0.2 fusion.39
  13.9 3.7 %fusion.4 = f32[128,4,768]{2,1,0:T(4,128)S(1)} fusion(f32[128,4,768]{2,1,0:T(4,128)S(1)} %get-tuple-element.9, f32[128,4,1]{2,1,0:T(4,128)S(1)} %get-tuple-element.17, f32[128,4,767]{2,1,0:T(4,128)S(1)} %get-tuple-element.19, f32[128,4,767]{2,1,0:T(4,128)S(1)} %get-tuple-element.18, f32[128,4,1]{2,1,0:T(4,128)S(1)} %get-tuple-element.16, ...), kind=kLoop, calls=%fused_computation.12 | loop fusion | flops 5898240 | bytes 9437184 | tf_op jit(solution)/shard_map/sub | solution.py:146
  17.6 1.6 %collective-permute-done = f32[128,2,768]{2,1,0:T(2,128)S(1)} collective-permute-done((f32[128,2,768]{2,1,0:T(2,128)S(1)}, f32[128,2,768]{2,1,0:T(2,128)S(1)}, u32[]{:S(2)}, u32[]{:S(2)}) %collective-permute-start) | collective-permute-done | bytes 786464 | tf_op jit(solution)/shard_map/ppermute | solution.py:26
  19.3 8.0 %collective-permute-done.1 = f32[128,2,768]{2,1,0:T(2,128)S(1)} collective-permute-done((f32[128,2,768]{2,1,0:T(2,128)S(1)}, f32[128,2,768]{2,1,0:T(2,128)S(1)}, u32[]{:S(2)}, u32[]{:S(2)}) %collective-permute-start.1) | collective-permute-done | bytes 786464 | tf_op jit(solution)/shard_map/ppermute | solution.py:25
  27.3 1.4 %fusion.10 = f32[128,4,768]{2,1,0:T(4,128)S(1)} fusion(f32[128,4,768]{2,1,0:T(4,128)S(1)} %fusion.4, f32[128,2,768]{2,1,0:T(2,128)S(1)} %collective-permute-done, f32[128,2,768]{2,1,0:T(2,128)S(1)} %collective-permute-done.1), kind=kLoop, calls=%fused_computation.18 | loop fusion | flops 2359296 | bytes 4718592 | tf_op jit(solution)/shard_map/add | solution.py:147
  28.7 1.7 %fusion.20 = f32[128,128]{1,0:T(8,128)S(1)} fusion(f32[128,4,768]{2,1,0:T(4,128)S(1)} %fusion.10), kind=kOutput, calls=%fused_computation.30 | convolution fusion | flops 603996160 | bytes 1638400 | tf_op jit(solution)/shard_map/dot_general | solution.py:150
  30.4 0.1 fusion.41
  30.5 0.1 select_maximum_fusion
  30.6 10.3 %all_to_all.20 = f32[8,65,128]{2,1,0:T(8,128)S(1)} all-to-all(f32[8,65,128]{2,1,0:T(8,128)S(1)} %broadcast_in_dim.52), channel_id=1, replica_groups=mesh['zh'=4,'zl'=4,'y'=4,'x'=4,'core'=2] {'x','core'}, dimensions={0} | all-to-all | bytes 532480 | tf_op jit(solution)/shard_map/all_to_all | solution.py:106
  40.9 8.4 %all_to_all.21 = f32[4,65,128]{2,1,0:T(8,128)S(1)} all-to-all(f32[4,65,128]{2,1,0:T(8,128)S(1)} %broadcast_in_dim.54), channel_id=1, replica_groups=mesh['zh'=4,'zl'=4,'y'=4,'x'=4,'core'=2] {'y'}, dimensions={0} | all-to-all | bytes 266240 | tf_op jit(solution)/shard_map/all_to_all | solution.py:106
  49.3 18.8 %all_to_all.22 = f32[4,65,128]{2,1,0:T(8,128)S(1)} all-to-all(f32[4,65,128]{2,1,0:T(8,128)S(1)} %broadcast_in_dim.56), channel_id=1, replica_groups=mesh['zh'=4,'zl'=4,'y'=4,'x'=4,'core'=2] {'zl'}, dimensions={0} | all-to-all | bytes 266240 | tf_op jit(solution)/shard_map/all_to_all | solution.py:106
  68.2 0.7 broadcast_in_dim.58
  68.8 5.6 %all-to-all-start.3 = ((f32[4,65,128]{2,1,0:T(8,128)}), f32[4,65,128]{2,1,0:T(8,128)S(1)}, u32[]{:S(2)}, u32[]{:S(2)}) async-start(f32[4,65,128]{2,1,0:T(8,128)} %broadcast_in_dim.58), calls=%async_computation.3 | async-start | bytes 294912 | tf_op jit(solution)/shard_map/all_to_all | solution.py:106
  74.4 0.3 copy.9
  74.7 0.5 copy.7
  75.1 13.5 %all-to-all-done.3 = f32[4,65,128]{2,1,0:T(8,128)S(1)} async-done(((f32[4,65,128]{2,1,0:T(8,128)}), f32[4,65,128]{2,1,0:T(8,128)S(1)}, u32[]{:S(2)}, u32[]{:S(2)}) %all-to-all-start.3) | async-done | bytes 133152 | tf_op jit(solution)/shard_map/all_to_all | solution.py:106
  88.7 0.1 slice.233
  88.7 0.1 copy.5
  88.8 0.1 bitcast_select_fusion.1
  88.9 0.1 copy.6
  89.0 0.7 maximum_maximum_fusion.gram_ref
  89.7 14.9 %shard_map.30 = (f32[128,128]{1,0:T(8,128)}, f32[128,128]{1,0:T(8,128)}) custom-call(f32[128,128]{1,0:T(8,128)} %maximum_maximum_fusion.gram_ref), custom_call_target="tpu_custom_call" | custom-call | tf_op jit(solution)/shard_map/pallas_call | solution.py:61
  104.6 2.3 %fusion.23 = f32[128,4,768]{2,0,1:T(8,128)S(1)} fusion(f32[4,768,128]{2,1,0:T(8,128)S(1)} %bitcast.36, f32[128,128]{1,0:T(8,128)} %get-tuple-element.4), kind=kOutput, calls=%fused_computation.32 | convolution fusion | flops 603979776 | bytes 3211264 | tf_op jit(solution)/shard_map/dot_general | solution.py:165
  107.0 2.2 %copy.8 = f32[128,4,768]{2,1,0:T(4,128)} copy(f32[128,4,768]{2,0,1:T(8,128)S(1)} %fusion.23) | data formatting | bytes 3145728
  (8 shorter events, 0.1 us)
Async XLA Ops:
  3.7 15.6 %collective-permute-start = (f32[128,2,768]{2,1,0:T(2,128)S(1)}, f32[128,2,768]{2,1,0:T(2,128)S(1)}, u32[]{:S(2)}, u32[]{:S(2)}) collective-permute-start(f32[128,2,768]{2,1,0:T(2,128)S(1)} %get-tuple-element.11), channel_id=1, source_target_pairs={{1,0},{2,1},{3,2},{4,3},{5,4},{6,5},{7,6},{8,7},{9,8},{10,9},{11,1... | collective-permute-start | bytes 2359304 | tf_op jit(solution)/shard_map/ppermute | solution.py:26
  9.8 17.5 %collective-permute-start.1 = (f32[128,2,768]{2,1,0:T(2,128)S(1)}, f32[128,2,768]{2,1,0:T(2,128)S(1)}, u32[]{:S(2)}, u32[]{:S(2)}) collective-permute-start(f32[128,2,768]{2,1,0:T(2,128)S(1)} %get-tuple-element.10), channel_id=1, source_target_pairs={{0,1},{1,2},{2,3},{3,4},{4,5},{5,6},{6,7},{7,8},{8,9},{9,10},{10,1... | collective-permute-start | bytes 2359304 | tf_op jit(solution)/shard_map/ppermute | solution.py:25
  68.8 19.8 %all-to-all-start.3 = ((f32[4,65,128]{2,1,0:T(8,128)}), f32[4,65,128]{2,1,0:T(8,128)S(1)}, u32[]{:S(2)}, u32[]{:S(2)}) async-start(f32[4,65,128]{2,1,0:T(8,128)} %broadcast_in_dim.58), calls=%async_computation.3 | async-start | bytes 294912 | tf_op jit(solution)/shard_map/all_to_all | solution.py:106
